TPU v7x, 128 devices: a whole 4x4x4 slice. The times are simulated.
128 devices in a mesh: gx: 4 (over z_lo, core), gy: 32 (over z_hi, x, y).
Axes of the slice: x: 4, y: 4, z: 4 (z_hi: 2, z_lo: 2; z = z_hi * 2 + z_lo), core: 2. Of those that a mesh axis runs over, the one named last changes fastest.
Arguments:
- hidden: bfloat16 [1024, 16384], P('gy'), may hold values from -6 to 6
- norm_gain: bfloat16 [16384], replicated, may hold values from 0.099609375 to 1.8984375
- w_query: bfloat16 [16384, 16384], P('gx', 'gy'), may hold values from -0.046875 to 0.046875
- w_keyval: bfloat16 [16384, 2048], P('gx', 'gy'), may hold values from -0.046875 to 0.046875
- key_cache: bfloat16 [1024, 256, 8, 128], P(('gx', 'gy')), may hold values from -1000 to 1000
- value_cache: bfloat16 [1024, 256, 8, 128], P(('gx', 'gy')), may hold values from -16 to 16
- lengths: int32 [1024], P(('gx', 'gy')), may hold values from 1 to 256, as said below
- w_out: bfloat16 [16384, 16384], P('gy', 'gx'), may hold values from -0.046875 to 0.046875
Outputs:
- mixed: bfloat16 [1024, 16384], P('gy', 'gx')
Inputs may be any that keep to these rules, and one draw needn't show every extreme that they name: Slots 0 to lengths - 1 of a row are filled; some row fills all 256.
All inputs are finite; a program needn't handle non-finite values.
Results may differ from a plain program's by a relative error of at most 0.024.
Values may be sent and summed in bfloat16 or wider, within the bound.
No kernel may reach another device: no remote copies, remote signals or barrier semaphores. Data moves between devices by JAX's collectives and lax.ppermute only.
A program may use at most 128 MiB of HBM per device.

v0:
```python
import math

import jax
import jax.numpy as jnp
from jax import lax
from jax.sharding import PartitionSpec as P


def rotate_heads(values, position, head_dim):
    half = head_dim // 2
    freq = jnp.exp(-(jnp.arange(half, dtype=jnp.float32) * 2.0 / head_dim) * math.log(500000.0))
    angle = position[:, None] * freq[None, :]
    cosine = jnp.cos(angle)[:, None, :]
    sine = jnp.sin(angle)[:, None, :]
    first = values[..., :half]
    second = values[..., half:]
    return jnp.concatenate(
        [first * cosine - second * sine, second * cosine + first * sine], axis=-1
    )


def attend_rows(query, keyval, key_cache, value_cache, lengths):
    rows, cache_len, kv_heads, head_dim = key_cache.shape
    heads = query.shape[1] // head_dim
    group = heads // kv_heads
    scale = 1.0 / math.sqrt(head_dim)
    position = lengths.astype(jnp.float32)
    rotated = rotate_heads(
        query.astype(jnp.float32).reshape(rows, heads, head_dim), position, head_dim
    ).astype(jnp.bfloat16)
    pairs = keyval.reshape(rows, 2, kv_heads, head_dim)
    new_key = rotate_heads(pairs[:, 0].astype(jnp.float32), position, head_dim).astype(jnp.bfloat16)
    new_value = pairs[:, 1].astype(jnp.float32)
    grouped = rotated.reshape(rows, kv_heads, group, head_dim)
    scores = (
        jnp.einsum("rgqd,rtgd->rgqt", grouped, key_cache, preferred_element_type=jnp.float32)
        * scale
    )
    own = jnp.einsum("rgqd,rgd->rgq", grouped, new_key, preferred_element_type=jnp.float32) * scale
    valid = jnp.arange(cache_len)[None, None, None, :] < lengths[:, None, None, None]
    scores = jnp.where(valid, scores, -jnp.inf)
    top = jnp.maximum(jnp.max(scores, axis=-1), own)
    weights = jnp.exp(scores - top[..., None])
    own_weight = jnp.exp(own - top)
    total = jnp.sum(weights, axis=-1) + own_weight
    probs = (weights / total[..., None]).astype(jnp.bfloat16)
    own_prob = (own_weight / total).astype(jnp.bfloat16)
    result = jnp.einsum("rgqt,rtgd->rgqd", probs, value_cache, preferred_element_type=jnp.float32)
    result = result + own_prob.astype(jnp.float32)[..., None] * new_value[:, :, None, :]
    return result.astype(jnp.bfloat16).reshape(rows, heads * head_dim)


def shards(hidden, norm_gain, w_query, w_keyval, key_cache, value_cache, lengths, w_out):
    width_part = w_query.shape[0]
    query_cols = w_query.shape[1]
    pair_cols = w_keyval.shape[1]
    peers = lax.axis_size("gy")
    values = hidden.astype(jnp.float32)
    inverse = lax.rsqrt(jnp.mean(values * values, axis=1, keepdims=True) + 1e-05)
    normed = (values * inverse * norm_gain.astype(jnp.float32)).astype(jnp.bfloat16)
    own_cols = lax.dynamic_slice_in_dim(normed, lax.axis_index("gx") * width_part, width_part, 1)
    gathered = lax.all_gather(own_cols, "gy", axis=0, tiled=True)
    summed = lax.psum_scatter(
        jnp.concatenate(
            [
                jnp.dot(gathered, w_query, preferred_element_type=jnp.float32),
                jnp.dot(gathered, w_keyval, preferred_element_type=jnp.float32),
            ],
            axis=1,
        ),
        "gx",
        scatter_dimension=0,
        tiled=True,
    )
    packed = summed.astype(jnp.bfloat16)
    local_qkv = lax.all_to_all(packed, "gy", split_axis=0, concat_axis=1, tiled=True)
    rows_dev = local_qkv.shape[0]
    split_cols = local_qkv.reshape(rows_dev, peers, query_cols + pair_cols)
    query = split_cols[:, :, :query_cols].reshape(rows_dev, peers * query_cols)
    keyval = split_cols[:, :, query_cols:].reshape(rows_dev, peers * pair_cols)
    attended = attend_rows(query, keyval, key_cache, value_cache, lengths)
    by_heads = lax.all_to_all(attended, "gy", split_axis=1, concat_axis=0, tiled=True)
    full_rows = lax.all_gather(by_heads, "gx", axis=0, tiled=True)
    partial_out = jnp.dot(full_rows, w_out, preferred_element_type=jnp.float32)
    result = lax.psum_scatter(
        partial_out.astype(jnp.bfloat16), "gy", scatter_dimension=0, tiled=True
    )
    return result


def solution(mesh):
    in_specs = (
        P("gy", None),
        P(),
        P("gx", "gy"),
        P("gx", "gy"),
        P(("gx", "gy"), None, None, None),
        P(("gx", "gy"), None, None, None),
        P(("gx", "gy")),
        P("gy", "gx"),
    )
    out_specs = P("gy", "gx")
    return jax.shard_map(shards, mesh=mesh, in_specs=in_specs, out_specs=out_specs, check_vma=False)
```

profile of v0, /device:TPU:0, one launch (start us, length us, event | category | flops | bytes accessed | tf_op | source)
XLA Modules:
  0.0 441.9 jit_solution(4741083174968831689)
XLA Ops:
  6.5 0.0 copy-start
  6.5 0.0 copy-start.2
  6.5 0.0 all-gather.3.cloned.1.call-start
  6.5 1.4 convert_element_type.56
  8.0 1.5 multiply_reduce_fusion
  9.5 0.0 copy-done.2
  9.6 0.8 fusion.18
  10.4 0.0 all-gather.3.cloned.1.call-update
  10.4 0.0 reduce-scatter.3.cloned.1.call-start
  10.5 107.1 %all-gather.3.cloned.1.call-done = bf16[1024,4096]{1,0:T(8,128)(2,1)} async-done(((bf16[32,4096]{1,0:T(8,128)(2,1)}), bf16[1024,4096]{1,0:T(8,128)(2,1)}) %all-gather.3.cloned.1.call-update) | async-done | bytes 8388624 | tf_op jit(solution)/shard_map/all_gather | solution.py:62
  117.5 0.0 copy-start.1
  117.5 8.4 %fusion.30 = f32[1024,512]{0,1:T(8,128)S(1)} fusion(bf16[1024,4096]{1,0:T(8,128)(2,1)} %all-gather.3.cloned.1.call-done, bf16[4096,512]{1,0:T(8,128)(2,1)} %param.10), kind=kOutput, calls=%fused_computation.45 | convolution fusion | flops 4294967296 | bytes 14680064 | tf_op jit(solution)/shard_map/dot_general | solution.py:66
  125.9 0.0 copy-done
  125.9 0.0 copy-done.1
  125.9 2.7 fusion.31
  128.6 0.0 copy-start.3
  128.6 1.7 pad_maximum_fusion
  130.3 0.0 reduce-scatter.3.cloned.1.call-update
  130.3 0.0 copy-done.3
  130.3 0.1 iota_compare_fusion
  130.4 28.1 %reduce-scatter.3.cloned.1.call-done = f32[256,576]{0,1:T(8,128)} async-done(((f32[1024,576]{0,1:T(8,128)}), f32[256,576]{0,1:T(8,128)}) %reduce-scatter.3.cloned.1.call-update) | async-done | bytes 589840 | tf_op jit(solution)/shard_map/reduce_scatter | solution.py:63
  158.4 1.1 convert_element_type.59
  159.5 0.9 copy.11
  160.4 9.4 %all-to-all-start = ((bf16[32,8,576]{2,1,0:T(8,128)(2,1)}), bf16[32,8,576]{2,1,0:T(8,128)(2,1)S(1)}, u32[]{:S(2)}, u32[]{:S(2)}) async-start(bf16[32,8,576]{2,1,0:T(8,128)(2,1)} %bitcast), calls=%async_computation.1 | async-start | bytes 655360 | tf_op jit(solution)/shard_map/all_to_all | solution.py:76
  169.8 0.0 all-gather.5.cloned.1.call-start
  169.9 0.1 multiply_cosine_fusion
  170.0 11.4 %all-to-all-done = bf16[32,8,576]{2,1,0:T(8,128)(2,1)S(1)} async-done(((bf16[32,8,576]{2,1,0:T(8,128)(2,1)}), bf16[32,8,576]{2,1,0:T(8,128)(2,1)S(1)}, u32[]{:S(2)}, u32[]{:S(2)}) %all-to-all-start) | async-done | bytes 294944 | tf_op jit(solution)/shard_map/all_to_all | solution.py:76
  181.5 0.1 reshape_reshape.3
  181.6 0.3 copy.12
  182.0 0.1 subtract_convert_fusion.1
  182.1 0.2 subtract_convert_fusion
  182.3 0.0 copy-start.4
  182.3 0.1 maximum_bitcast_fusion
  182.4 0.3 fusion.21
  182.7 3.7 fusion.29
  186.5 0.4 fusion.16
  186.9 0.0 copy-done.4
  186.9 1.0 fusion.13
  187.9 0.2 all_to_all.29
  188.1 0.2 copy.16
  188.3 14.5 %all_to_all.35 = bf16[8,32,512]{2,0,1:T(8,128)(2,1)} all-to-all(bf16[8,32,512]{2,0,1:T(8,128)(2,1)S(1)} %copy.16), channel_id=1, replica_groups=mesh['gx'=4,'gy'=32] {'gy'}, dimensions={1} | all-to-all | bytes 524288 | tf_op jit(solution)/shard_map/all_to_all | solution.py:82
  202.7 0.0 all-gather.5.cloned.1.call-update
  202.7 0.2 reduce-scatter.5.cloned.1.call-start
  203.0 15.7 %all-gather.5.cloned.1.call-done = bf16[1024,512]{1,0:T(8,128)(2,1)} async-done(((bf16[256,512]{1,0:T(8,128)(2,1)}), bf16[1024,512]{1,0:T(8,128)(2,1)}) %all-gather.5.cloned.1.call-update) | async-done | bytes 1048592 | tf_op jit(solution)/shard_map/all_gather | solution.py:83
  218.6 10.3 %convolution_convert_fusion = bf16[1024,4096]{1,0:T(8,128)(2,1)} fusion(bf16[1024,512]{1,0:T(8,128)(2,1)} %all-gather.5.cloned.1.call-done, bf16[512,4096]{1,0:T(8,128)(2,1)} %param.15), kind=kOutput, calls=%fused_computation | convolution fusion | flops 4299161600 | bytes 13631488 | tf_op jit(solution)/shard_map/dot_general | solution.py:84
  228.9 0.0 reduce-scatter.5.cloned.1.call-update
  228.9 206.5 %reduce-scatter.5.cloned.1.call-done = bf16[32,4096]{1,0:T(8,128)(2,1)} async-done(((bf16[1024,4096]{1,0:T(8,128)(2,1)}), bf16[32,4096]{1,0:T(8,128)(2,1)}) %reduce-scatter.5.cloned.1.call-update) | async-done | bytes 262160 | tf_op jit(solution)/shard_map/reduce_scatter | solution.py:85
  (11 shorter events, 0.2 us)
Async XLA Ops:
  6.5 119.4 %copy-start = (bf16[4096,64]{0,1:T(8,128)(2,1)S(1)}, bf16[4096,64]{0,1:T(8,128)(2,1)}, u32[]{:S(2)}) copy-start(bf16[4096,64]{0,1:T(8,128)(2,1)} %param.11) | copy-start | bytes 1572868
  6.5 3.0 copy-start.2
  6.5 111.0 %all-gather.3.cloned.1.call-start = ((), (), s32[]{:S(2)}) async-start(), calls=%async_computation.4 | async-start | bytes 8650752 | tf_op jit(solution)/shard_map/all_gather | solution.py:62
  10.4 148.0 %reduce-scatter.3.cloned.1.call-start = ((), (), s32[]{:S(2)}) async-start(), calls=%async_computation.5 | async-start | bytes 2949120 | tf_op jit(solution)/shard_map/reduce_scatter | solution.py:63
  117.5 8.4 %copy-start.1 = (bf16[1024,4096]{1,0:T(8,128)(2,1)S(1)}, bf16[1024,4096]{1,0:T(8,128)(2,1)}, u32[]{:S(2)}) copy-start(bf16[1024,4096]{1,0:T(8,128)(2,1)} %all-gather.3.cloned.1.call-done) | copy-start | bytes 25165828
  128.6 1.7 copy-start.3
  160.4 21.0 %all-to-all-start = ((bf16[32,8,576]{2,1,0:T(8,128)(2,1)}), bf16[32,8,576]{2,1,0:T(8,128)(2,1)S(1)}, u32[]{:S(2)}, u32[]{:S(2)}) async-start(bf16[32,8,576]{2,1,0:T(8,128)(2,1)} %bitcast), calls=%async_computation.1 | async-start | bytes 655360 | tf_op jit(solution)/shard_map/all_to_all | solution.py:76
  169.8 48.8 %all-gather.5.cloned.1.call-start = ((), (), s32[]{:S(2)}) async-start(), calls=%async_computation.6 | async-start | bytes 1310720 | tf_op jit(solution)/shard_map/all_gather | solution.py:83
  182.3 4.6 %copy-start.4 = (bf16[8,256,8,128]{3,2,1,0:T(8,128)(2,1)S(1)}, bf16[8,256,8,128]{3,2,1,0:T(8,128)(2,1)}, u32[]{:S(2)}) copy-start(bf16[8,256,8,128]{3,2,1,0:T(8,128)(2,1)} %param.13) | copy-start | bytes 12582916
  202.7 232.6 %reduce-scatter.5.cloned.1.call-start = ((), (), s32[]{:S(2)}) async-start(), calls=%async_computation.7 | async-start | bytes 8650752 | tf_op jit(solution)/shard_map/reduce_scatter | solution.py:85
Sparse Core Ops, SparseCore 0:
  10.5 106.9 all-gather.2
  130.4 27.9 reduce-scatter.2
  202.9 15.7 all-gather.4
  229.0 206.2 reduce-scatter.4
where the time goes:
time: 442 us
  waiting for transfers between devices  369 us (83%)
  matrix products  26.3 us (6%)
  blocking collectives  14.5 us (3%)
  between operations  13.3 us (3%)
  starting transfers between devices  9.68 us (2%)
  other arithmetic  7.66 us (2%)
    reduce_scatter x1, waiting for transfers between devices, shards(): lax.psum_scatter(partial_out.astype(jnp.bfloat16), 'gy', scatter_dimensio...  206 us
    all_gather x1, waiting for transfers between devices, shards(): gathered = lax.all_gather(own_cols, 'gy', axis=0, tiled=True)  107 us
    reduce_scatter x1, waiting for transfers between devices, shards(): lax.psum_scatter(jnp.concatenate([jnp.dot(gathered, w_query, preferred_el...  28.1 us
    all_gather x1, waiting for transfers between devices, shards(): full_rows = lax.all_gather(by_heads, 'gx', axis=0, tiled=True)  15.7 us
    all_to_all x1, blocking collectives, shards(): lax.all_to_all(attended, 'gy', split_axis=1, concat_axis=0, tiled=True)  14.5 us
    all_to_all x1, waiting for transfers between devices, shards(): lax.all_to_all(packed, 'gy', split_axis=0, concat_axis=1, tiled=True)  11.4 us
    dot_general x1, matrix products, shards(): partial_out = jnp.dot(full_rows, w_out, preferred_element_type=jnp.float32)  10.3 us
    all_to_all x1, starting transfers between devices, shards(): lax.all_to_all(packed, 'gy', split_axis=0, concat_axis=1, tiled=True)  9.37 us
  transfers between devices with their start and end apart: 5, of which 5 were waited for; matrix products, arithmetic and copies ran while one was open for 0% of the time, Pallas kernels for 0%

commit v1 on v0

--- a/solution.py
+++ b/solution.py
@@ -4,6 +4,8 @@
 import jax.numpy as jnp
 from jax import lax
 from jax.sharding import PartitionSpec as P
+
+GY = ("zh", "x", "y")
 
 
 def rotate_heads(values, position, head_dim):
@@ -54,12 +56,12 @@
     width_part = w_query.shape[0]
     query_cols = w_query.shape[1]
     pair_cols = w_keyval.shape[1]
-    peers = lax.axis_size("gy")
+    peers = 32
     values = hidden.astype(jnp.float32)
     inverse = lax.rsqrt(jnp.mean(values * values, axis=1, keepdims=True) + 1e-05)
     normed = (values * inverse * norm_gain.astype(jnp.float32)).astype(jnp.bfloat16)
     own_cols = lax.dynamic_slice_in_dim(normed, lax.axis_index("gx") * width_part, width_part, 1)
-    gathered = lax.all_gather(own_cols, "gy", axis=0, tiled=True)
+    gathered = lax.all_gather(own_cols, GY, axis=0, tiled=True)
     summed = lax.psum_scatter(
         jnp.concatenate(
             [
@@ -73,31 +75,37 @@
         tiled=True,
     )
     packed = summed.astype(jnp.bfloat16)
-    local_qkv = lax.all_to_all(packed, "gy", split_axis=0, concat_axis=1, tiled=True)
+    local_qkv = lax.all_to_all(packed, GY, split_axis=0, concat_axis=1, tiled=True)
     rows_dev = local_qkv.shape[0]
     split_cols = local_qkv.reshape(rows_dev, peers, query_cols + pair_cols)
     query = split_cols[:, :, :query_cols].reshape(rows_dev, peers * query_cols)
     keyval = split_cols[:, :, query_cols:].reshape(rows_dev, peers * pair_cols)
     attended = attend_rows(query, keyval, key_cache, value_cache, lengths)
-    by_heads = lax.all_to_all(attended, "gy", split_axis=1, concat_axis=0, tiled=True)
+    by_heads = lax.all_to_all(attended, GY, split_axis=1, concat_axis=0, tiled=True)
     full_rows = lax.all_gather(by_heads, "gx", axis=0, tiled=True)
+    full_rows = full_rows.reshape(2, 4, 4, -1, full_rows.shape[1]).transpose(2, 1, 0, 3, 4)
+    full_rows = full_rows.reshape(-1, full_rows.shape[-1])
     partial_out = jnp.dot(full_rows, w_out, preferred_element_type=jnp.float32)
-    result = lax.psum_scatter(
-        partial_out.astype(jnp.bfloat16), "gy", scatter_dimension=0, tiled=True
-    )
-    return result
+    part = partial_out.astype(jnp.bfloat16)
+    rows, cols = part.shape
+    part = lax.psum_scatter(part, "y", scatter_dimension=0, tiled=True)
+    part = lax.psum_scatter(part, "x", scatter_dimension=0, tiled=True)
+    part = lax.psum_scatter(part, "zh", scatter_dimension=0, tiled=True)
+    return part.reshape(rows // 32, cols)
 
 
 def solution(mesh):
+    from jax.sharding import Mesh
+    mesh = Mesh(mesh.devices.reshape(4, 2, 4, 4), ("gx", "zh", "x", "y"))
     in_specs = (
-        P("gy", None),
+        P(GY, None),
         P(),
-        P("gx", "gy"),
-        P("gx", "gy"),
-        P(("gx", "gy"), None, None, None),
-        P(("gx", "gy"), None, None, None),
-        P(("gx", "gy")),
-        P("gy", "gx"),
+        P("gx", GY),
+        P("gx", GY),
+        P(("gx",) + GY, None, None, None),
+        P(("gx",) + GY, None, None, None),
+        P(("gx",) + GY),
+        P(GY, "gx"),
     )
-    out_specs = P("gy", "gx")
+    out_specs = P(GY, "gx")
     return jax.shard_map(shards, mesh=mesh, in_specs=in_specs, out_specs=out_specs, check_vma=False)

time: 442 us -> 371 us (0.84)
  waiting for transfers between devices: 369 us -> 297 us
    reduce_scatter x1 -> x3, waiting for transfers between devices: 206 us -> 134 us  [the longest x1 82 us: shards(): part = lax.psum_scatter(part, 'y', scatter_dimension=0, tiled=True)]
  transfers between devices with their start and end apart: 5 -> 7, of which waited for: 5 -> 7; matrix products, arithmetic and copies ran while one was open for 0% -> 0% of each run, Pallas kernels for 0% -> 0%
where the time goes in v1:
time: 371 us; the launch traced here: 370 us
  waiting for transfers between devices  297 us (80%)
  matrix products  25 us (7%)
  blocking collectives  14.5 us (4%)
  between operations  13.7 us (4%)
  starting transfers between devices  9.58 us (3%)
  other arithmetic  7.66 us (2%)
    all_gather x1, waiting for transfers between devices, shards(): gathered = lax.all_gather(own_cols, GY, axis=0, tiled=True)  107 us
    reduce_scatter x1, waiting for transfers between devices, shards(): part = lax.psum_scatter(part, 'y', scatter_dimension=0, tiled=True)  82 us
    reduce_scatter x1, waiting for transfers between devices, shards(): part = lax.psum_scatter(part, 'x', scatter_dimension=0, tiled=True)  31.6 us
    reduce_scatter x1, waiting for transfers between devices, shards(): lax.psum_scatter(jnp.concatenate([jnp.dot(gathered, w_query, preferred_el...  28.1 us
    reduce_scatter x1, waiting for transfers between devices, shards(): part = lax.psum_scatter(part, 'zh', scatter_dimension=0, tiled=True)  20.8 us
    all_gather x1, waiting for transfers between devices, shards(): full_rows = lax.all_gather(by_heads, 'gx', axis=0, tiled=True)  15.8 us
    all_to_all x1, blocking collectives, shards(): lax.all_to_all(attended, GY, split_axis=1, concat_axis=0, tiled=True)  14.5 us
    all_to_all x1, waiting for transfers between devices, shards(): lax.all_to_all(packed, GY, split_axis=0, concat_axis=1, tiled=True)  11.4 us
  transfers between devices with their start and end apart: 7, of which 7 were waited for; matrix products, arithmetic and copies ran while one was open for 0% of the time, Pallas kernels for 0%

profile of v1, /device:TPU:0, one launch (start us, length us, event | category | flops | bytes accessed | tf_op | source)
XLA Modules:
  0.0 370.2 jit_solution(14718961935474674799)
XLA Ops:
  6.5 0.0 copy-start
  6.5 0.0 copy-start.2
  6.5 0.0 all-gather.3.cloned.1.call-start
  6.5 1.4 convert_element_type.56
  8.0 1.5 multiply_reduce_fusion
  9.5 0.0 copy-done.2
  9.6 0.8 fusion.18
  10.4 0.0 all-gather.3.cloned.1.call-update
  10.4 0.0 reduce-scatter.5.cloned.1.call-start
  10.5 107.1 %all-gather.3.cloned.1.call-done = bf16[1024,4096]{1,0:T(8,128)(2,1)} async-done(((bf16[32,4096]{1,0:T(8,128)(2,1)}), bf16[1024,4096]{1,0:T(8,128)(2,1)}) %all-gather.3.cloned.1.call-update) | async-done | bytes 8388624 | tf_op jit(solution)/shard_map/all_gather | solution.py:64
  117.5 0.0 copy-start.1
  117.5 8.4 %fusion.30 = f32[1024,512]{0,1:T(8,128)S(1)} fusion(bf16[1024,4096]{1,0:T(8,128)(2,1)} %all-gather.3.cloned.1.call-done, bf16[4096,512]{1,0:T(8,128)(2,1)} %param.10), kind=kOutput, calls=%fused_computation.45 | convolution fusion | flops 4294967296 | bytes 14680064 | tf_op jit(solution)/shard_map/dot_general | solution.py:68
  125.9 0.0 copy-done
  125.9 0.0 copy-done.1
  125.9 2.7 fusion.31
  128.6 0.0 copy-start.3
  128.6 1.7 pad_maximum_fusion
  130.3 0.0 reduce-scatter.5.cloned.1.call-update
  130.3 0.0 copy-done.3
  130.3 0.1 iota_compare_fusion
  130.4 28.1 %reduce-scatter.5.cloned.1.call-done = f32[256,576]{0,1:T(8,128)} async-done(((f32[1024,576]{0,1:T(8,128)}), f32[256,576]{0,1:T(8,128)}) %reduce-scatter.5.cloned.1.call-update) | async-done | bytes 589840 | tf_op jit(solution)/shard_map/reduce_scatter | solution.py:65
  158.4 1.1 convert_element_type.59
  159.5 0.9 copy.11
  160.4 9.4 %all-to-all-start = ((bf16[32,8,576]{2,1,0:T(8,128)(2,1)}), bf16[32,8,576]{2,1,0:T(8,128)(2,1)S(1)}, u32[]{:S(2)}, u32[]{:S(2)}) async-start(bf16[32,8,576]{2,1,0:T(8,128)(2,1)} %bitcast), calls=%async_computation.1 | async-start | bytes 655360 | tf_op jit(solution)/shard_map/all_to_all | solution.py:78
  169.8 0.0 all-gather.5.cloned.1.call-start
  169.9 0.1 multiply_cosine_fusion
  170.0 11.4 %all-to-all-done = bf16[32,8,576]{2,1,0:T(8,128)(2,1)S(1)} async-done(((bf16[32,8,576]{2,1,0:T(8,128)(2,1)}), bf16[32,8,576]{2,1,0:T(8,128)(2,1)S(1)}, u32[]{:S(2)}, u32[]{:S(2)}) %all-to-all-start) | async-done | bytes 294944 | tf_op jit(solution)/shard_map/all_to_all | solution.py:78
  181.5 0.1 reshape_reshape.3
  181.6 0.3 copy.12
  182.0 0.1 subtract_convert_fusion.1
  182.1 0.2 subtract_convert_fusion
  182.3 0.0 copy-start.4
  182.3 0.1 maximum_bitcast_fusion
  182.4 0.3 fusion.21
  182.7 3.7 %fusion.29 = (f32[8,8,16]{2,1,0:T(8,128)S(1)}, f32[8,8,16,256]{3,2,1,0:T(8,128)S(1)}) fusion(bf16[8,256,8,128]{3,2,1,0:T(8,128)(2,1)} %param.12, bf16[8,8,16,64]{3,2,1,0:T(8,128)(2,1)S(1)} %bitcast.41, bf16[8,8,16,64]{3,2,1,0:T(8,128)(2,1)S(1)} %bitcast.39, pred[8,256]{1,0:T(8,128)(4,1)S(1)} %iota_compare_fusion), kind=kOutput, calls=%fused_computation.44 | convolution fusion | flops 68418560 | bytes 5511168 | tf_op jit(solution)/shard_map/rgqd,rtgd->rgqt/dot_general | solution.py:38
  186.5 0.4 fusion.16
  186.9 0.0 copy-done.4
  186.9 1.0 fusion.13
  187.9 0.2 all_to_all.29
  188.1 0.2 copy.16
  188.3 14.5 %all_to_all.35 = bf16[8,32,512]{2,0,1:T(8,128)(2,1)} all-to-all(bf16[8,32,512]{2,0,1:T(8,128)(2,1)S(1)} %copy.16), channel_id=1, replica_groups=mesh['gx'=4,'zh'=2,'x'=4,'y'=4] {'zh','x','y'}, dimensions={1} | all-to-all | bytes 524288 | tf_op jit(solution)/shard_map/all_to_all | solution.py:84
  202.7 0.0 all-gather.5.cloned.1.call-update
  202.7 0.0 reduce-scatter.7.cloned.1.call-start
  202.8 15.8 %all-gather.5.cloned.1.call-done = bf16[1024,512]{1,0:T(8,128)(2,1)} async-done(((bf16[256,512]{1,0:T(8,128)(2,1)}), bf16[1024,512]{1,0:T(8,128)(2,1)}) %all-gather.5.cloned.1.call-update) | async-done | bytes 1048592 | tf_op jit(solution)/shard_map/all_gather | solution.py:85
  218.6 1.3 copy.17
  219.9 8.9 %convolution_convert_fusion = bf16[1024,4096]{1,0:T(8,128)(2,1)} fusion(bf16[1024,512]{1,0:T(8,128)(2,1)S(1)} %bitcast.36, bf16[512,4096]{1,0:T(8,128)(2,1)} %param.15), kind=kOutput, calls=%fused_computation | convolution fusion | flops 4299161600 | bytes 13631488 | tf_op jit(solution)/shard_map/dot_general | solution.py:88
  228.8 0.0 reduce-scatter.7.cloned.1.call-update
  228.9 0.0 reduce-scatter.9.cloned.1.call-start
  228.9 82.0 %reduce-scatter.7.cloned.1.call-done = bf16[256,4096]{1,0:T(8,128)(2,1)} async-done(((bf16[1024,4096]{1,0:T(8,128)(2,1)}), bf16[256,4096]{1,0:T(8,128)(2,1)}) %reduce-scatter.7.cloned.1.call-update) | async-done | bytes 2097168 | tf_op jit(solution)/shard_map/reduce_scatter | solution.py:91
  310.9 0.0 reduce-scatter.9.cloned.1.call-update
  310.9 0.0 reduce-scatter.11.cloned.1.call-start
  310.9 31.6 %reduce-scatter.9.cloned.1.call-done = bf16[64,4096]{1,0:T(8,128)(2,1)} async-done(((bf16[256,4096]{1,0:T(8,128)(2,1)}), bf16[64,4096]{1,0:T(8,128)(2,1)}) %reduce-scatter.9.cloned.1.call-update) | async-done | bytes 524304 | tf_op jit(solution)/shard_map/reduce_scatter | solution.py:92
  342.5 0.0 reduce-scatter.11.cloned.1.call-update
  342.6 20.8 %reduce-scatter.11.cloned.1.call-done = bf16[32,4096]{1,0:T(8,128)(2,1)} async-done(((bf16[64,4096]{1,0:T(8,128)(2,1)}), bf16[32,4096]{1,0:T(8,128)(2,1)}) %reduce-scatter.11.cloned.1.call-update) | async-done | bytes 262160 | tf_op jit(solution)/shard_map/reduce_scatter | solution.py:93
  (11 shorter events, 0.2 us)
Async XLA Ops:
  6.5 119.4 %copy-start = (bf16[4096,64]{0,1:T(8,128)(2,1)S(1)}, bf16[4096,64]{0,1:T(8,128)(2,1)}, u32[]{:S(2)}) copy-start(bf16[4096,64]{0,1:T(8,128)(2,1)} %param.11) | copy-start | bytes 1572868
  6.5 3.0 copy-start.2
  6.5 111.0 %all-gather.3.cloned.1.call-start = ((), (), s32[]{:S(2)}) async-start(), calls=%async_computation.6 | async-start | bytes 8650752 | tf_op jit(solution)/shard_map/all_gather | solution.py:64
  10.4 148.0 %reduce-scatter.5.cloned.1.call-start = ((), (), s32[]{:S(2)}) async-start(), calls=%async_computation.7 | async-start | bytes 2949120 | tf_op jit(solution)/shard_map/reduce_scatter | solution.py:65
  117.5 8.4 %copy-start.1 = (bf16[1024,4096]{1,0:T(8,128)(2,1)S(1)}, bf16[1024,4096]{1,0:T(8,128)(2,1)}, u32[]{:S(2)}) copy-start(bf16[1024,4096]{1,0:T(8,128)(2,1)} %all-gather.3.cloned.1.call-done) | copy-start | bytes 25165828
  128.6 1.7 copy-start.3
  160.4 21.0 %all-to-all-start = ((bf16[32,8,576]{2,1,0:T(8,128)(2,1)}), bf16[32,8,576]{2,1,0:T(8,128)(2,1)S(1)}, u32[]{:S(2)}, u32[]{:S(2)}) async-start(bf16[32,8,576]{2,1,0:T(8,128)(2,1)} %bitcast), calls=%async_computation.1 | async-start | bytes 655360 | tf_op jit(solution)/shard_map/all_to_all | solution.py:78
  169.8 48.8 %all-gather.5.cloned.1.call-start = ((), (), s32[]{:S(2)}) async-start(), calls=%async_computation.8 | async-start | bytes 1310720 | tf_op jit(solution)/shard_map/all_gather | solution.py:85
  182.3 4.6 %copy-start.4 = (bf16[8,256,8,128]{3,2,1,0:T(8,128)(2,1)S(1)}, bf16[8,256,8,128]{3,2,1,0:T(8,128)(2,1)}, u32[]{:S(2)}) copy-start(bf16[8,256,8,128]{3,2,1,0:T(8,128)(2,1)} %param.13) | copy-start | bytes 12582916
  202.7 108.1 %reduce-scatter.7.cloned.1.call-start = ((), (), s32[]{:S(2)}) async-start(), calls=%async_computation.9 | async-start | bytes 10485760 | tf_op jit(solution)/shard_map/reduce_scatter | solution.py:91
  228.9 113.7 %reduce-scatter.9.cloned.1.call-start = ((), (), s32[]{:S(2)}) async-start(), calls=%async_computation.10 | async-start | bytes 2621440 | tf_op jit(solution)/shard_map/reduce_scatter | solution.py:92
  310.9 52.4 %reduce-scatter.11.cloned.1.call-start = ((), (), s32[]{:S(2)}) async-start(), calls=%async_computation.11 | async-start | bytes 786432 | tf_op jit(solution)/shard_map/reduce_scatter | solution.py:93
Sparse Core Ops, SparseCore 0:
  10.5 106.9 all-gather.2
  130.4 27.9 reduce-scatter.4
  202.9 15.7 all-gather.4
  229.0 81.8 reduce-scatter.6
  313.1 29.3 reduce-scatter.8
  344.7 18.5 reduce-scatter.10

commit v2 on v1

--- a/solution.py
+++ b/solution.py
@@ -61,19 +61,18 @@
     inverse = lax.rsqrt(jnp.mean(values * values, axis=1, keepdims=True) + 1e-05)
     normed = (values * inverse * norm_gain.astype(jnp.float32)).astype(jnp.bfloat16)
     own_cols = lax.dynamic_slice_in_dim(normed, lax.axis_index("gx") * width_part, width_part, 1)
-    gathered = lax.all_gather(own_cols, GY, axis=0, tiled=True)
-    summed = lax.psum_scatter(
-        jnp.concatenate(
-            [
-                jnp.dot(gathered, w_query, preferred_element_type=jnp.float32),
-                jnp.dot(gathered, w_keyval, preferred_element_type=jnp.float32),
-            ],
-            axis=1,
-        ),
-        "gx",
-        scatter_dimension=0,
-        tiled=True,
+    gathered = lax.all_gather(own_cols, "zh", axis=0, tiled=True)
+    gathered = lax.all_gather(gathered, ("x", "y"), axis=0, tiled=True)
+    projected = jnp.concatenate(
+        [
+            jnp.dot(gathered, w_query, preferred_element_type=jnp.float32),
+            jnp.dot(gathered, w_keyval, preferred_element_type=jnp.float32),
+        ],
+        axis=1,
     )
+    projected = projected.reshape(4, 4, 2, -1, projected.shape[1]).transpose(2, 0, 1, 3, 4)
+    projected = projected.reshape(-1, projected.shape[-1])
+    summed = lax.psum_scatter(projected, "gx", scatter_dimension=0, tiled=True)
     packed = summed.astype(jnp.bfloat16)
     local_qkv = lax.all_to_all(packed, GY, split_axis=0, concat_axis=1, tiled=True)
     rows_dev = local_qkv.shape[0]
@@ -83,15 +82,12 @@
     attended = attend_rows(query, keyval, key_cache, value_cache, lengths)
     by_heads = lax.all_to_all(attended, GY, split_axis=1, concat_axis=0, tiled=True)
     full_rows = lax.all_gather(by_heads, "gx", axis=0, tiled=True)
-    full_rows = full_rows.reshape(2, 4, 4, -1, full_rows.shape[1]).transpose(2, 1, 0, 3, 4)
-    full_rows = full_rows.reshape(-1, full_rows.shape[-1])
     partial_out = jnp.dot(full_rows, w_out, preferred_element_type=jnp.float32)
     part = partial_out.astype(jnp.bfloat16)
     rows, cols = part.shape
-    part = lax.psum_scatter(part, "y", scatter_dimension=0, tiled=True)
-    part = lax.psum_scatter(part, "x", scatter_dimension=0, tiled=True)
-    part = lax.psum_scatter(part, "zh", scatter_dimension=0, tiled=True)
-    return part.reshape(rows // 32, cols)
+    part = lax.all_to_all(part, GY, split_axis=0, concat_axis=0, tiled=True)
+    part = part.reshape(peers, rows // peers, cols).astype(jnp.float32).sum(axis=0)
+    return part.astype(jnp.bfloat16)
 
 
 def solution(mesh):

time: 371 us -> 330 us (0.89)
  waiting for transfers between devices: 297 us -> 132 us
  blocking collectives: 14.5 us -> 132 us
  other arithmetic: 7.66 us -> 13.7 us
    reduce_scatter x4 -> x1, waiting for transfers between devices: 162 us -> 32.2 us  [shards(): summed = lax.psum_scatter(projected, 'gx', scatter_dimension=0, tiled=True)]
    all_to_all x0 -> x1, blocking collectives: none -> 106 us  [shards(): part = lax.all_to_all(part, GY, split_axis=0, concat_axis=0, tiled=True)]
    all_gather x1, waiting for transfers between devices: 107 us -> 72.5 us  [shards(): gathered = lax.all_gather(gathered, ('x', 'y'), axis=0, tiled=True)]
    all_gather x0 -> x1, blocking collectives: none -> 11.1 us  [shards(): gathered = lax.all_gather(own_cols, 'zh', axis=0, tiled=True)]
    reduce_sum x0 -> x1, other arithmetic: none -> 5.94 us  [shards(): part.reshape(peers, rows // peers, cols).astype(jnp.float32).sum(axis=0)]
  transfers between devices with their start and end apart: 7 -> 4, of which waited for: 7 -> 4; matrix products, arithmetic and copies ran while one was open for 0% -> 0% of each run, Pallas kernels for 0% -> 0%
where the time goes in v2:
time: 330 us
  blocking collectives  132 us (40%)
  waiting for transfers between devices  132 us (40%)
  matrix products  24.8 us (8%)
  other arithmetic  13.7 us (4%)
  between operations  13.3 us (4%)
  starting transfers between devices  9.47 us (3%)
  local copies, waits for them, and re-layouts  4.66 us (1%)
    all_to_all x1, blocking collectives, shards(): part = lax.all_to_all(part, GY, split_axis=0, concat_axis=0, tiled=True)  106 us
    all_gather x1, waiting for transfers between devices, shards(): gathered = lax.all_gather(gathered, ('x', 'y'), axis=0, tiled=True)  72.5 us
    reduce_scatter x1, waiting for transfers between devices, shards(): summed = lax.psum_scatter(projected, 'gx', scatter_dimension=0, tiled=True)  32.2 us
    all_gather x1, waiting for transfers between devices, shards(): full_rows = lax.all_gather(by_heads, 'gx', axis=0, tiled=True)  15.9 us
    all_to_all x1, blocking collectives, shards(): lax.all_to_all(attended, GY, split_axis=1, concat_axis=0, tiled=True)  14.5 us
    all_to_all x1, waiting for transfers between devices, shards(): lax.all_to_all(packed, GY, split_axis=0, concat_axis=1, tiled=True)  11.4 us
    all_gather x1, blocking collectives, shards(): gathered = lax.all_gather(own_cols, 'zh', axis=0, tiled=True)  11.1 us
    all_to_all x1, starting transfers between devices, shards(): lax.all_to_all(packed, GY, split_axis=0, concat_axis=1, tiled=True)  9.39 us
  transfers between devices with their start and end apart: 4, of which 4 were waited for; matrix products, arithmetic and copies ran while one was open for 0% of the time, Pallas kernels for 0%

profile of v2, /device:TPU:0, one launch (start us, length us, event | category | flops | bytes accessed | tf_op | source)
XLA Modules:
  0.0 329.9 jit_solution(1639970296449035327)
XLA Ops:
  6.5 0.0 copy-start
  6.5 0.0 copy-start.2
  6.5 0.0 all-gather.3.cloned.1.call-start
  6.5 1.6 multiply_reduce_fusion
  8.1 1.4 convert_element_type.58
  9.5 0.0 copy-done.2
  9.6 0.1 fusion.18
  9.7 11.1 %all_gather.9 = bf16[64,4096]{1,0:T(8,128)(2,1)} all-gather(bf16[32,4096]{1,0:T(8,128)(2,1)S(1)} %fusion.18), channel_id=1, replica_groups=mesh['gx'=4,'zh'=2,'x'=4,'y'=4] {'zh'}, dimensions={0}, use_global_device_ids=true | all-gather | bytes 786432 | tf_op jit(solution)/shard_map/all_gather | solution.py:64
  20.7 0.0 all-gather.3.cloned.1.call-update
  20.8 0.0 reduce-scatter.2.cloned.1.call-start
  20.8 72.5 %all-gather.3.cloned.1.call-done = bf16[1024,4096]{1,0:T(8,128)(2,1)} async-done(((bf16[64,4096]{1,0:T(8,128)(2,1)}), bf16[1024,4096]{1,0:T(8,128)(2,1)}) %all-gather.3.cloned.1.call-update) | async-done | bytes 8388624 | tf_op jit(solution)/shard_map/all_gather | solution.py:65
  93.3 0.0 copy-done
  93.3 0.0 copy-start.1
  93.3 6.2 %fusion.31 = f32[1024,64]{0,1:T(8,128)S(1)} fusion(bf16[1024,4096]{1,0:T(8,128)(2,1)} %all-gather.3.cloned.1.call-done, bf16[4096,64]{0,1:T(8,128)(2,1)S(1)} %copy-done), kind=kOutput, calls=%fused_computation.47 | convolution fusion | flops 536870912 | bytes 9175040 | tf_op jit(solution)/shard_map/dot_general | solution.py:69
  99.5 0.0 copy-done.1
  99.5 6.5 %fusion.30 = f32[1024,512]{0,1:T(8,128)S(1)} fusion(bf16[1024,4096]{1,0:T(8,128)(2,1)S(1)} %copy-done.1, bf16[4096,512]{1,0:T(8,128)(2,1)} %param.10), kind=kOutput, calls=%fused_computation.46 | convolution fusion | flops 4294967296 | bytes 14680064 | tf_op jit(solution)/shard_map/dot_general | solution.py:68
  106.0 1.7 pad_maximum_fusion
  107.7 2.1 copy.17
  109.8 0.0 copy-start.3
  109.8 1.7 copy.18
  111.6 0.0 reduce-scatter.2.cloned.1.call-update
  111.6 0.0 copy-done.3
  111.6 0.1 iota_compare_fusion
  111.7 32.2 %reduce-scatter.2.cloned.1.call-done = f32[256,576]{1,0:T(8,128)} async-done(((f32[1024,576]{1,0:T(8,128)}), f32[256,576]{1,0:T(8,128)}) %reduce-scatter.2.cloned.1.call-update) | async-done | bytes 589840 | tf_op jit(solution)/shard_map/reduce_scatter | solution.py:75
  143.9 1.8 convert_bitcast_fusion
  145.8 9.4 %all-to-all-start = ((bf16[32,8,576]{2,1,0:T(8,128)(2,1)}), bf16[32,8,576]{2,1,0:T(8,128)(2,1)S(1)}, u32[]{:S(2)}, u32[]{:S(2)}) async-start(bf16[32,8,576]{2,1,0:T(8,128)(2,1)} %convert_bitcast_fusion), calls=%async_computation.1 | async-start | bytes 655360 | tf_op jit(solution)/shard_map/all_to_all | solution.py:77
  155.2 0.0 all-gather.5.cloned.1.call-start
  155.2 0.1 multiply_cosine_fusion
  155.4 11.4 %all-to-all-done = bf16[32,8,576]{2,1,0:T(8,128)(2,1)S(1)} async-done(((bf16[32,8,576]{2,1,0:T(8,128)(2,1)}), bf16[32,8,576]{2,1,0:T(8,128)(2,1)S(1)}, u32[]{:S(2)}, u32[]{:S(2)}) %all-to-all-start) | async-done | bytes 294944 | tf_op jit(solution)/shard_map/all_to_all | solution.py:77
  166.9 0.1 reshape_reshape.3
  167.0 0.3 copy.19
  167.3 0.1 subtract_convert_fusion.1
  167.4 0.2 subtract_convert_fusion
  167.7 0.0 copy-start.4
  167.7 0.1 maximum_bitcast_fusion
  167.8 0.3 fusion.21
  168.1 3.7 %fusion.29 = (f32[8,8,16]{2,1,0:T(8,128)S(1)}, f32[8,8,16,256]{3,2,1,0:T(8,128)S(1)}) fusion(bf16[8,256,8,128]{3,2,1,0:T(8,128)(2,1)} %param.12, bf16[8,8,16,64]{3,2,1,0:T(8,128)(2,1)S(1)} %bitcast.44, bf16[8,8,16,64]{3,2,1,0:T(8,128)(2,1)S(1)} %bitcast.42, pred[8,256]{1,0:T(8,128)(4,1)S(1)} %iota_compare_fusion), kind=kOutput, calls=%fused_computation.45 | convolution fusion | flops 68418560 | bytes 5511168 | tf_op jit(solution)/shard_map/rgqd,rtgd->rgqt/dot_general | solution.py:38
  171.8 0.4 fusion.16
  172.3 0.0 copy-done.4
  172.3 1.0 fusion.13
  173.3 0.2 all_to_all.35
  173.5 0.2 copy.23
  173.6 14.5 %all_to_all.44 = bf16[8,32,512]{2,0,1:T(8,128)(2,1)} all-to-all(bf16[8,32,512]{2,0,1:T(8,128)(2,1)S(1)} %copy.23), channel_id=1, replica_groups=mesh['gx'=4,'zh'=2,'x'=4,'y'=4] {'zh','x','y'}, dimensions={1} | all-to-all | bytes 524288 | tf_op jit(solution)/shard_map/all_to_all | solution.py:83
  188.1 0.0 all-gather.5.cloned.1.call-update
  188.1 15.9 %all-gather.5.cloned.1.call-done = bf16[1024,512]{1,0:T(8,128)(2,1)} async-done(((bf16[256,512]{1,0:T(8,128)(2,1)}), bf16[1024,512]{1,0:T(8,128)(2,1)}) %all-gather.5.cloned.1.call-update) | async-done | bytes 1048592 | tf_op jit(solution)/shard_map/all_gather | solution.py:84
  204.0 7.0 %convolution_convert_fusion = bf16[1024,4096]{1,0:T(8,128)(2,1)S(1)} fusion(bf16[1024,512]{1,0:T(8,128)(2,1)} %all-gather.5.cloned.1.call-done, bf16[512,4096]{1,0:T(8,128)(2,1)} %param.15), kind=kOutput, calls=%fused_computation | convolution fusion | flops 4299161600 | bytes 13631488 | tf_op jit(solution)/shard_map/dot_general | solution.py:85
  211.0 106.4 %all_to_all.45 = bf16[32,32,4096]{2,1,0:T(8,128)(2,1)} all-to-all(bf16[32,32,4096]{2,1,0:T(8,128)(2,1)S(1)} %bitcast.37), channel_id=1, replica_groups=mesh['gx'=4,'zh'=2,'x'=4,'y'=4] {'zh','x','y'}, dimensions={0} | all-to-all | bytes 16777216 | tf_op jit(solution)/shard_map/all_to_all | solution.py:88
  317.4 5.9 %reduce_sum.32 = bf16[32,4096]{1,0:T(8,128)(2,1)} reduce(bf16[32,32,4096]{2,1,0:T(8,128)(2,1)} %all_to_all.45, bf16[]{:T(256)} %constant.32.clone.1), dimensions={0}, to_apply=%region_4.5 | reduce | flops 4063232 | bytes 8650754 | tf_op jit(solution)/shard_map/reduce_sum | solution.py:89
  (11 shorter events, 0.2 us)
Async XLA Ops:
  6.5 86.8 %copy-start = (bf16[4096,64]{0,1:T(8,128)(2,1)S(1)}, bf16[4096,64]{0,1:T(8,128)(2,1)}, u32[]{:S(2)}) copy-start(bf16[4096,64]{0,1:T(8,128)(2,1)} %param.11) | copy-start | bytes 1572868
  6.5 3.0 copy-start.2
  6.5 86.8 %all-gather.3.cloned.1.call-start = ((), (), s32[]{:S(2)}) async-start(), calls=%async_computation.4 | async-start | bytes 8912896 | tf_op jit(solution)/shard_map/all_gather | solution.py:65
  20.8 123.2 %reduce-scatter.2.cloned.1.call-start = ((), (), s32[]{:S(2)}) async-start(), calls=%async_computation.5 | async-start | bytes 3276800 | tf_op jit(solution)/shard_map/reduce_scatter | solution.py:75
  93.3 6.2 %copy-start.1 = (bf16[1024,4096]{1,0:T(8,128)(2,1)S(1)}, bf16[1024,4096]{1,0:T(8,128)(2,1)}, u32[]{:S(2)}) copy-start(bf16[1024,4096]{1,0:T(8,128)(2,1)} %all-gather.3.cloned.1.call-done) | copy-start | bytes 25165828
  109.8 1.8 copy-start.3
  145.8 21.0 %all-to-all-start = ((bf16[32,8,576]{2,1,0:T(8,128)(2,1)}), bf16[32,8,576]{2,1,0:T(8,128)(2,1)S(1)}, u32[]{:S(2)}, u32[]{:S(2)}) async-start(bf16[32,8,576]{2,1,0:T(8,128)(2,1)} %convert_bitcast_fusion), calls=%async_computation.1 | async-start | bytes 655360 | tf_op jit(solution)/shard_map/all_to_all | solution.py:77
  155.2 48.8 %all-gather.5.cloned.1.call-start = ((), (), s32[]{:S(2)}) async-start(), calls=%async_computation.6 | async-start | bytes 1310720 | tf_op jit(solution)/shard_map/all_gather | solution.py:84
  167.7 4.6 %copy-start.4 = (bf16[8,256,8,128]{3,2,1,0:T(8,128)(2,1)S(1)}, bf16[8,256,8,128]{3,2,1,0:T(8,128)(2,1)}, u32[]{:S(2)}) copy-start(bf16[8,256,8,128]{3,2,1,0:T(8,128)(2,1)} %param.13) | copy-start | bytes 12582916
Sparse Core Ops, SparseCore 0:
  20.9 72.4 all-gather.2
  111.7 32.1 reduce-scatter.1
  188.2 15.7 all-gather.4

commit v3 on v2

--- a/solution.py
+++ b/solution.py
@@ -6,6 +6,7 @@
 from jax.sharding import PartitionSpec as P
 
 GY = ("zh", "x", "y")
+ALL = ("gx",) + GY
 
 
 def rotate_heads(values, position, head_dim):
@@ -72,16 +73,16 @@
     )
     projected = projected.reshape(4, 4, 2, -1, projected.shape[1]).transpose(2, 0, 1, 3, 4)
     projected = projected.reshape(-1, projected.shape[-1])
-    summed = lax.psum_scatter(projected, "gx", scatter_dimension=0, tiled=True)
-    packed = summed.astype(jnp.bfloat16)
-    local_qkv = lax.all_to_all(packed, GY, split_axis=0, concat_axis=1, tiled=True)
-    rows_dev = local_qkv.shape[0]
-    split_cols = local_qkv.reshape(rows_dev, peers, query_cols + pair_cols)
+    arrived = lax.all_to_all(projected, ALL, split_axis=0, concat_axis=0, tiled=True)
+    rows_dev = arrived.shape[0] // 128
+    summed = arrived.reshape(4, peers, rows_dev, query_cols + pair_cols).sum(axis=0)
+    split_cols = summed.astype(jnp.bfloat16).transpose(1, 0, 2)
     query = split_cols[:, :, :query_cols].reshape(rows_dev, peers * query_cols)
     keyval = split_cols[:, :, query_cols:].reshape(rows_dev, peers * pair_cols)
     attended = attend_rows(query, keyval, key_cache, value_cache, lengths)
-    by_heads = lax.all_to_all(attended, GY, split_axis=1, concat_axis=0, tiled=True)
-    full_rows = lax.all_gather(by_heads, "gx", axis=0, tiled=True)
+    heads_first = attended.reshape(rows_dev, peers, query_cols).transpose(1, 0, 2)
+    sent = jnp.broadcast_to(heads_first[None], (4,) + heads_first.shape).reshape(-1, query_cols)
+    full_rows = lax.all_to_all(sent, ALL, split_axis=0, concat_axis=0, tiled=True)
     partial_out = jnp.dot(full_rows, w_out, preferred_element_type=jnp.float32)
     part = partial_out.astype(jnp.bfloat16)
     rows, cols = part.shape

time: 330 us -> 308 us (0.933)
  waiting for transfers between devices: 132 us -> 107 us
  blocking collectives: 132 us -> 137 us
    reduce_scatter x1 -> x0, waiting for transfers between devices: 32.2 us -> none  [shards(): summed = lax.psum_scatter(projected, 'gx', scatter_dimension=0, tiled=True)]
    all_to_all x1, waiting for transfers between devices: 11.4 us -> 34.7 us  [shards(): lax.all_to_all(projected, ALL, split_axis=0, concat_axis=0, tiled=True)]
    all_gather x1 -> x0, waiting for transfers between devices: 15.9 us -> none  [shards(): full_rows = lax.all_gather(by_heads, 'gx', axis=0, tiled=True)]
    all_to_all x1, blocking collectives: 14.5 us -> 23.9 us  [shards(): lax.all_to_all(sent, ALL, split_axis=0, concat_axis=0, tiled=True)]
    all_to_all x1, blocking collectives: 106 us -> 102 us  [shards(): part = lax.all_to_all(part, GY, split_axis=0, concat_axis=0, tiled=True)]
  transfers between devices with their start and end apart: 4 -> 2, of which waited for: 4 -> 2; matrix products, arithmetic and copies ran while one was open for 0% -> 0% of each run, Pallas kernels for 0% -> 0%
where the time goes in v3:
time: 308 us; the launch traced here: 307 us
  blocking collectives  137 us (44%)
  waiting for transfers between devices  107 us (35%)
  matrix products  24.6 us (8%)
  between operations  13.6 us (4%)
  other arithmetic  12 us (4%)
  starting transfers between devices  8.39 us (3%)
  local copies, waits for them, and re-layouts  4.73 us (2%)
    all_to_all x1, blocking collectives, shards(): part = lax.all_to_all(part, GY, split_axis=0, concat_axis=0, tiled=True)  102 us
    all_gather x1, waiting for transfers between devices, shards(): gathered = lax.all_gather(gathered, ('x', 'y'), axis=0, tiled=True)  72.6 us
    all_to_all x1, waiting for transfers between devices, shards(): lax.all_to_all(projected, ALL, split_axis=0, concat_axis=0, tiled=True)  34.7 us
    all_to_all x1, blocking collectives, shards(): lax.all_to_all(sent, ALL, split_axis=0, concat_axis=0, tiled=True)  23.9 us
    all_gather x1, blocking collectives, shards(): gathered = lax.all_gather(own_cols, 'zh', axis=0, tiled=True)  11.1 us
    all_to_all x1, starting transfers between devices, shards(): lax.all_to_all(projected, ALL, split_axis=0, concat_axis=0, tiled=True)  8.39 us
    dot_general x1, matrix products, shards(): partial_out = jnp.dot(full_rows, w_out, preferred_element_type=jnp.float32)  6.91 us
    dot_general x1, matrix products, shards(): jnp.dot(gathered, w_query, preferred_element_type=jnp.float32)  6.49 us
  transfers between devices with their start and end apart: 2, of which 2 were waited for; matrix products, arithmetic and copies ran while one was open for 0% of the time, Pallas kernels for 0%

profile of v3, /device:TPU:0, one launch (start us, length us, event | category | flops | bytes accessed | tf_op | source)
XLA Modules:
  0.0 307.4 jit_solution(14021811710843776462)
XLA Ops:
  6.5 0.0 copy-start
  6.5 0.0 copy-start.2
  6.5 0.0 all-gather.2.cloned.1.call-start
  6.5 1.6 multiply_reduce_fusion
  8.1 1.4 convert_element_type.62
  9.5 0.0 copy-done.2
  9.6 0.1 fusion.19
  9.7 11.1 %all_gather.6 = bf16[64,4096]{1,0:T(8,128)(2,1)} all-gather(bf16[32,4096]{1,0:T(8,128)(2,1)S(1)} %fusion.19), channel_id=1, replica_groups=mesh['gx'=4,'zh'=2,'x'=4,'y'=4] {'zh'}, dimensions={0}, use_global_device_ids=true | all-gather | bytes 786432 | tf_op jit(solution)/shard_map/all_gather | solution.py:65
  20.7 0.0 all-gather.2.cloned.1.call-update
  20.8 72.6 %all-gather.2.cloned.1.call-done = bf16[1024,4096]{1,0:T(8,128)(2,1)} async-done(((bf16[64,4096]{1,0:T(8,128)(2,1)}), bf16[1024,4096]{1,0:T(8,128)(2,1)}) %all-gather.2.cloned.1.call-update) | async-done | bytes 8388624 | tf_op jit(solution)/shard_map/all_gather | solution.py:66
  93.3 0.0 copy-done
  93.3 0.0 copy-start.1
  93.3 6.2 %fusion.32 = f32[1024,64]{0,1:T(8,128)S(1)} fusion(bf16[1024,4096]{1,0:T(8,128)(2,1)} %all-gather.2.cloned.1.call-done, bf16[4096,64]{0,1:T(8,128)(2,1)S(1)} %copy-done), kind=kOutput, calls=%fused_computation.48 | convolution fusion | flops 536870912 | bytes 9175040 | tf_op jit(solution)/shard_map/dot_general | solution.py:70
  99.5 0.0 copy-done.1
  99.5 6.5 %fusion.31 = f32[1024,512]{0,1:T(8,128)S(1)} fusion(bf16[1024,4096]{1,0:T(8,128)(2,1)S(1)} %copy-done.1, bf16[4096,512]{1,0:T(8,128)(2,1)} %param.10), kind=kOutput, calls=%fused_computation.47 | convolution fusion | flops 4294967296 | bytes 14680064 | tf_op jit(solution)/shard_map/dot_general | solution.py:69
  106.0 1.7 pad_maximum_fusion
  107.7 2.1 copy.23
  109.8 0.0 copy-start.3
  109.9 1.7 copy.24
  111.6 8.4 %all-to-all-start = ((f32[128,8,576]{2,1,0:T(8,128)}), f32[128,8,576]{2,1,0:T(8,128)S(1)}, u32[]{:S(2)}, u32[]{:S(2)}) async-start(f32[128,8,576]{2,1,0:T(8,128)} %bitcast.38), calls=%async_computation | async-start | bytes 5242880 | tf_op jit(solution)/shard_map/all_to_all | solution.py:76
  120.0 0.0 copy-done.3
  120.0 0.1 iota_compare_fusion
  120.1 0.1 multiply_cosine_fusion
  120.2 34.7 %all-to-all-done = f32[128,8,576]{2,1,0:T(8,128)S(1)} async-done(((f32[128,8,576]{2,1,0:T(8,128)}), f32[128,8,576]{2,1,0:T(8,128)S(1)}, u32[]{:S(2)}, u32[]{:S(2)}) %all-to-all-start) | async-done | bytes 2359328 | tf_op jit(solution)/shard_map/all_to_all | solution.py:76
  154.9 0.2 reduce_sum.40
  155.1 0.1 slice_convert_fusion
  155.2 0.1 reshape_reshape.6
  155.3 0.3 copy.25
  155.7 0.1 subtract_convert_fusion.1
  155.7 0.2 subtract_convert_fusion
  156.0 0.0 copy-start.4
  156.0 0.1 maximum_bitcast_fusion
  156.1 0.3 fusion.22
  156.4 3.7 %fusion.30 = (f32[8,8,16]{2,1,0:T(8,128)S(1)}, f32[8,8,16,256]{3,2,1,0:T(8,128)S(1)}) fusion(bf16[8,256,8,128]{3,2,1,0:T(8,128)(2,1)} %param.12, bf16[8,8,16,64]{3,2,1,0:T(8,128)(2,1)S(1)} %bitcast.48, bf16[8,8,16,64]{3,2,1,0:T(8,128)(2,1)S(1)} %bitcast.46, pred[8,256]{1,0:T(8,128)(4,1)S(1)} %iota_compare_fusion), kind=kOutput, calls=%fused_computation.46 | convolution fusion | flops 68418560 | bytes 5511168 | tf_op jit(solution)/shard_map/rgqd,rtgd->rgqt/dot_general | solution.py:39
  160.1 0.4 fusion.17
  160.6 0.0 copy-done.4
  160.6 1.0 fusion.13
  161.6 0.2 reshape_reshape.7
  161.8 0.2 copy.29
  161.9 0.1 broadcast_in_dim.12
  162.0 23.9 %all_to_all.30 = bf16[128,8,512]{2,1,0:T(8,128)(2,1)S(1)} all-to-all(bf16[128,8,512]{2,1,0:T(8,128)(2,1)S(1)} %bitcast.41), channel_id=1, replica_groups=mesh['gx'=4,'zh'=2,'x'=4,'y'=4] {'gx','zh','x','y'}, dimensions={0} | all-to-all | bytes 2097152 | tf_op jit(solution)/shard_map/all_to_all | solution.py:85
  185.9 6.9 %convolution_convert_fusion = bf16[1024,4096]{1,0:T(8,128)(2,1)S(1)} fusion(bf16[512,4096]{1,0:T(8,128)(2,1)} %param.15, bf16[128,8,512]{2,1,0:T(8,128)(2,1)S(1)} %all_to_all.30), kind=kOutput, calls=%fused_computation | convolution fusion | flops 4299161600 | bytes 13631488 | tf_op jit(solution)/shard_map/dot_general | solution.py:86
  192.8 101.8 %all_to_all.31 = bf16[32,32,4096]{2,1,0:T(8,128)(2,1)} all-to-all(bf16[32,32,4096]{2,1,0:T(8,128)(2,1)S(1)} %bitcast.40), channel_id=1, replica_groups=mesh['gx'=4,'zh'=2,'x'=4,'y'=4] {'zh','x','y'}, dimensions={0} | all-to-all | bytes 16777216 | tf_op jit(solution)/shard_map/all_to_all | solution.py:89
  294.6 5.9 %reduce_sum.42 = bf16[32,4096]{1,0:T(8,128)(2,1)} reduce(bf16[32,32,4096]{2,1,0:T(8,128)(2,1)} %all_to_all.31, bf16[]{:T(256)} %constant.32.clone.1), dimensions={0}, to_apply=%region_4.5 | reduce | flops 4063232 | bytes 8650754 | tf_op jit(solution)/shard_map/reduce_sum | solution.py:90
  (10 shorter events, 0.1 us)
Async XLA Ops:
  6.5 86.8 %copy-start = (bf16[4096,64]{0,1:T(8,128)(2,1)S(1)}, bf16[4096,64]{0,1:T(8,128)(2,1)}, u32[]{:S(2)}) copy-start(bf16[4096,64]{0,1:T(8,128)(2,1)} %param.11) | copy-start | bytes 1572868
  6.5 3.0 copy-start.2
  6.5 86.8 %all-gather.2.cloned.1.call-start = ((), (), s32[]{:S(2)}) async-start(), calls=%async_computation.3 | async-start | bytes 8912896 | tf_op jit(solution)/shard_map/all_gather | solution.py:66
  93.3 6.2 %copy-start.1 = (bf16[1024,4096]{1,0:T(8,128)(2,1)S(1)}, bf16[1024,4096]{1,0:T(8,128)(2,1)}, u32[]{:S(2)}) copy-start(bf16[1024,4096]{1,0:T(8,128)(2,1)} %all-gather.2.cloned.1.call-done) | copy-start | bytes 25165828
  109.8 10.2 %copy-start.3 = (s32[8]{0:T(128)S(1)}, s32[8]{0:T(128)}, u32[]{:S(2)}) copy-start(s32[8]{0:T(128)} %param.14) | copy-start | bytes 100
  111.6 43.3 %all-to-all-start = ((f32[128,8,576]{2,1,0:T(8,128)}), f32[128,8,576]{2,1,0:T(8,128)S(1)}, u32[]{:S(2)}, u32[]{:S(2)}) async-start(f32[128,8,576]{2,1,0:T(8,128)} %bitcast.38), calls=%async_computation | async-start | bytes 5242880 | tf_op jit(solution)/shard_map/all_to_all | solution.py:76
  156.0 4.6 %copy-start.4 = (bf16[8,256,8,128]{3,2,1,0:T(8,128)(2,1)S(1)}, bf16[8,256,8,128]{3,2,1,0:T(8,128)(2,1)}, u32[]{:S(2)}) copy-start(bf16[8,256,8,128]{3,2,1,0:T(8,128)(2,1)} %param.13) | copy-start | bytes 12582916
Sparse Core Ops, SparseCore 0:
  20.9 72.4 all-gather.1

commit v4 on v3

--- a/solution.py
+++ b/solution.py
@@ -53,6 +53,24 @@
     return result.astype(jnp.bfloat16).reshape(rows, heads * head_dim)
 
 
+def ring_reduce_scatter(arr, axis, dim):
+    n = arr.shape[dim]
+    idx = lax.axis_index(axis)
+    half = arr.shape[-1] // 2
+    cw, ccw = arr[..., :half], arr[..., half:]
+
+    def take(a, k):
+        return lax.dynamic_index_in_dim(a, k % n, dim, keepdims=False)
+
+    fwd = [(i, (i + 1) % n) for i in range(n)]
+    bwd = [(i, (i - 1) % n) for i in range(n)]
+    acc_cw, acc_ccw = take(cw, idx - 1), take(ccw, idx + 1)
+    for s in range(n - 1):
+        acc_cw = lax.ppermute(acc_cw, axis, fwd) + take(cw, idx - s - 2)
+        acc_ccw = lax.ppermute(acc_ccw, axis, bwd) + take(ccw, idx + s + 2)
+    return jnp.concatenate([acc_cw, acc_ccw], axis=-1)
+
+
 def shards(hidden, norm_gain, w_query, w_keyval, key_cache, value_cache, lengths, w_out):
     width_part = w_query.shape[0]
     query_cols = w_query.shape[1]
@@ -73,9 +91,9 @@
     )
     projected = projected.reshape(4, 4, 2, -1, projected.shape[1]).transpose(2, 0, 1, 3, 4)
     projected = projected.reshape(-1, projected.shape[-1])
-    arrived = lax.all_to_all(projected, ALL, split_axis=0, concat_axis=0, tiled=True)
+    arrived = lax.all_to_all(projected.astype(jnp.bfloat16), ALL, split_axis=0, concat_axis=0, tiled=True)
     rows_dev = arrived.shape[0] // 128
-    summed = arrived.reshape(4, peers, rows_dev, query_cols + pair_cols).sum(axis=0)
+    summed = arrived.reshape(4, peers, rows_dev, query_cols + pair_cols).astype(jnp.float32).sum(axis=0)
     split_cols = summed.astype(jnp.bfloat16).transpose(1, 0, 2)
     query = split_cols[:, :, :query_cols].reshape(rows_dev, peers * query_cols)
     keyval = split_cols[:, :, query_cols:].reshape(rows_dev, peers * pair_cols)
@@ -86,9 +104,15 @@
     partial_out = jnp.dot(full_rows, w_out, preferred_element_type=jnp.float32)
     part = partial_out.astype(jnp.bfloat16)
     rows, cols = part.shape
-    part = lax.all_to_all(part, GY, split_axis=0, concat_axis=0, tiled=True)
-    part = part.reshape(peers, rows // peers, cols).astype(jnp.float32).sum(axis=0)
-    return part.astype(jnp.bfloat16)
+    part = part.reshape(2, 4, 4, rows // peers, cols)
+    first, second = part[..., : cols // 2], part[..., cols // 2 :]
+    first = ring_reduce_scatter(first, "y", 2)
+    second = ring_reduce_scatter(second, "x", 1)
+    first = ring_reduce_scatter(first, "x", 1)
+    second = ring_reduce_scatter(second, "y", 1)
+    first = ring_reduce_scatter(first, "zh", 0)
+    second = ring_reduce_scatter(second, "zh", 0)
+    return jnp.concatenate([first, second], axis=-1)
 
 
 def solution(mesh):

time: 308 us -> 267 us (0.87)
  blocking collectives: 137 us -> 11.1 us
  starting transfers between devices: 8.39 us -> 62.2 us
  waiting for transfers between devices: 107 us -> 134 us
  local copies, waits for them, and re-layouts: 4.73 us -> 12 us
  other arithmetic: 12 us -> 8.55 us
    all_to_all x2 -> x0, blocking collectives: 126 us -> none  [the longest x1 102 us: shards(): part = lax.all_to_all(part, GY, split_axis=0, concat_axis=0, tiled=True)]
    ppermute x0 -> x28, starting transfers between devices: none -> 48.5 us  [the longest x14 45.9 us: ring_reduce_scatter(): acc_ccw = lax.ppermute(acc_ccw, axis, bwd) + take(ccw, idx + s + 2)]
    ppermute x0 -> x28, waiting for transfers between devices: none -> 23.3 us  [the longest x14 22.6 us: ring_reduce_scatter(): acc_cw = lax.ppermute(acc_cw, axis, fwd) + take(cw, idx - s - 2)]
    reduce_sum x2 -> x1, other arithmetic: 6.1 us -> 0.35 us  [shards(): arrived.reshape(4, peers, rows_dev, query_cols + pair_cols)]
    all_to_all x1 -> x2, starting transfers between devices: 8.39 us -> 13.8 us  [the longest x1 8.39 us: shards(): lax.all_to_all(projected.astype(jnp.bfloat16), ALL, split_axis=0, concat_...]
    squeeze x0 -> x12, local copies, waits for them, and re-layouts: none -> 4.08 us  [take(): return lax.dynamic_index_in_dim(a, k % n, dim, keepdims=False)]
    all_to_all x1 -> x2, waiting for transfers between devices: 34.7 us -> 38.4 us  [the longest x1 20.6 us: shards(): lax.all_to_all(projected.astype(jnp.bfloat16), ALL, split_axis=0, concat_...]
    dot_general x1, matrix products: 6.19 us -> 2.66 us  [shards(): jnp.dot(gathered, w_keyval, preferred_element_type=jnp.float32)]
  transfers between devices with their start and end apart: 2 -> 31, of which waited for: 2 -> 13; matrix products, arithmetic and copies ran while one was open for 0% -> 2% of each run, Pallas kernels for 0% -> 0%
where the time goes in v4:
time: 267 us; the launch traced here: 266 us
  waiting for transfers between devices  134 us (50%)
  starting transfers between devices  62.2 us (23%)
  matrix products  23.8 us (9%)
  between operations  14.1 us (5%)
  local copies, waits for them, and re-layouts  12 us (4%)
  blocking collectives  11.1 us (4%)
  other arithmetic  8.55 us (3%)
    all_gather x1, waiting for transfers between devices, shards(): gathered = lax.all_gather(gathered, ('x', 'y'), axis=0, tiled=True)  72.6 us
    ppermute x14, starting transfers between devices, ring_reduce_scatter(): acc_ccw = lax.ppermute(acc_ccw, axis, bwd) + take(ccw, idx + s + 2)  45.9 us
    ppermute x14, waiting for transfers between devices, ring_reduce_scatter(): acc_cw = lax.ppermute(acc_cw, axis, fwd) + take(cw, idx - s - 2)  22.6 us
    all_to_all x1, waiting for transfers between devices, shards(): lax.all_to_all(projected.astype(jnp.bfloat16), ALL, split_axis=0, concat_...  20.6 us
    all_to_all x1, waiting for transfers between devices, shards(): lax.all_to_all(sent, ALL, split_axis=0, concat_axis=0, tiled=True)  17.8 us
    all_gather x1, blocking collectives, shards(): gathered = lax.all_gather(own_cols, 'zh', axis=0, tiled=True)  11.1 us
    dot_general x1, matrix products, shards(): jnp.dot(gathered, w_query, preferred_element_type=jnp.float32)  9.25 us
    all_to_all x1, starting transfers between devices, shards(): lax.all_to_all(projected.astype(jnp.bfloat16), ALL, split_axis=0, concat_...  8.39 us
  transfers between devices with their start and end apart: 31, of which 13 were waited for; matrix products, arithmetic and copies ran while one was open for 2% of the time, Pallas kernels for 0%

profile of v4, /device:TPU:0, one launch (start us, length us, event | category | flops | bytes accessed | tf_op | source)
XLA Modules:
  0.0 266.0 jit_solution(5929142238255258639)
XLA Ops:
  6.5 2.8 %convert_element_type.66 = f32[32,16384]{1,0:T(8,128)} convert(bf16[32,16384]{1,0:T(8,128)(2,1)} %param.8) | non-fusion elementwise | flops 524288 | bytes 3145728 | tf_op jit(solution)/shard_map/convert_element_type | solution.py:79
  9.4 0.3 multiply_reduce_fusion
  9.7 1.2 fusion.19
  10.9 11.1 %all_gather.6 = bf16[64,4096]{1,0:T(8,128)(2,1)} all-gather(bf16[32,4096]{1,0:T(8,128)(2,1)S(1)} %fusion.19), channel_id=1, replica_groups=mesh['gx'=4,'zh'=2,'x'=4,'y'=4] {'zh'}, dimensions={0}, use_global_device_ids=true | all-gather | bytes 786432 | tf_op jit(solution)/shard_map/all_gather | solution.py:83
  22.0 72.6 %all-gather.2.cloned.1.call-done = bf16[1024,4096]{1,0:T(8,128)(2,1)} async-done(((bf16[64,4096]{1,0:T(8,128)(2,1)}), bf16[1024,4096]{1,0:T(8,128)(2,1)}) %all-gather.2.cloned.1.call-update) | async-done | bytes 8388624 | tf_op jit(solution)/shard_map/all_gather | solution.py:84
  94.6 9.2 %convolution_convert_fusion.1 = bf16[1024,512]{0,1:T(8,128)(2,1)S(1)} fusion(bf16[1024,4096]{1,0:T(8,128)(2,1)} %all-gather.2.cloned.1.call-done, bf16[4096,512]{1,0:T(8,128)(2,1)} %param.10), kind=kOutput, calls=%fused_computation.6 | convolution fusion | flops 4295491584 | bytes 13631488 | tf_op jit(solution)/shard_map/dot_general | solution.py:87
  103.8 2.7 convolution_convert_fusion.2
  106.5 0.1 pad_maximum_fusion
  106.6 0.7 copy.23
  107.3 1.3 copy.24
  108.6 8.4 %all-to-all-start = ((bf16[128,8,576]{2,1,0:T(8,128)(2,1)}), bf16[128,8,576]{2,1,0:T(8,128)(2,1)S(1)}, u32[]{:S(2)}, u32[]{:S(2)}) async-start(bf16[128,8,576]{2,1,0:T(8,128)(2,1)} %bitcast.2), calls=%async_computation | async-start | bytes 2621440 | tf_op jit(solution)/shard_map/all_to_all | solution.py:94
  117.1 0.1 multiply_cosine_fusion
  117.2 20.6 %all-to-all-done = bf16[128,8,576]{2,1,0:T(8,128)(2,1)S(1)} async-done(((bf16[128,8,576]{2,1,0:T(8,128)(2,1)}), bf16[128,8,576]{2,1,0:T(8,128)(2,1)S(1)}, u32[]{:S(2)}, u32[]{:S(2)}) %all-to-all-start) | async-done | bytes 1179680 | tf_op jit(solution)/shard_map/all_to_all | solution.py:94
  137.8 0.4 reduce_sum.31
  138.2 0.1 reshape_reshape.6
  138.3 0.3 copy.25
  138.7 0.1 subtract_convert_fusion.1
  138.8 0.2 subtract_convert_fusion
  139.0 0.1 maximum_bitcast_fusion
  139.1 0.3 fusion.22
  139.4 3.7 %fusion.31 = (f32[8,8,16]{2,1,0:T(8,128)S(1)}, f32[8,8,16,256]{3,2,1,0:T(8,128)S(1)}) fusion(bf16[8,256,8,128]{3,2,1,0:T(8,128)(2,1)} %param.12, bf16[8,8,16,64]{3,2,1,0:T(8,128)(2,1)S(1)} %bitcast.124, bf16[8,8,16,64]{3,2,1,0:T(8,128)(2,1)S(1)} %bitcast.122, pred[8,256]{1,0:T(8,128)(4,1)S(1)} %iota_compare_fusion), kind=kOutput, calls=%fused_computation.89 | convolution fusion | flops 68418560 | bytes 5511168 | tf_op jit(solution)/shard_map/rgqd,rtgd->rgqt/dot_general | solution.py:39
  143.1 0.4 fusion.17
  143.6 1.0 fusion.13
  144.5 0.2 reshape_reshape.7
  144.7 0.2 copy.29
  144.9 1.1 broadcast_in_dim.12
  145.9 5.4 %all-to-all-start.1 = ((bf16[128,8,512]{2,1,0:T(8,128)(2,1)}), bf16[128,8,512]{2,1,0:T(8,128)(2,1)S(1)}, u32[]{:S(2)}, u32[]{:S(2)}) async-start(bf16[128,8,512]{2,1,0:T(8,128)(2,1)} %bitcast.14), calls=%async_computation.1 | async-start | bytes 2097152 | tf_op jit(solution)/shard_map/all_to_all | solution.py:103
  151.3 17.8 %all-to-all-done.1 = bf16[128,8,512]{2,1,0:T(8,128)(2,1)S(1)} async-done(((bf16[128,8,512]{2,1,0:T(8,128)(2,1)}), bf16[128,8,512]{2,1,0:T(8,128)(2,1)S(1)}, u32[]{:S(2)}, u32[]{:S(2)}) %all-to-all-start.1) | async-done | bytes 1048608 | tf_op jit(solution)/shard_map/all_to_all | solution.py:103
  169.2 6.9 %convolution_convert_fusion = bf16[1024,4096]{1,0:T(8,128)(2,1)S(1)} fusion(bf16[512,4096]{1,0:T(8,128)(2,1)} %param.15, bf16[128,8,512]{2,1,0:T(8,128)(2,1)S(1)} %all-to-all-done.1), kind=kOutput, calls=%fused_computation | convolution fusion | flops 4299161600 | bytes 13631488 | tf_op jit(solution)/shard_map/dot_general | solution.py:104
  176.1 2.7 %fusion.30 = (bf16[2,4,4,32,1024]{4,3,2,1,0:T(8,128)(2,1)S(1)}, bf16[2,4,4,32,1024]{4,3,2,1,0:T(8,128)(2,1)S(1)}, bf16[2,4,4,32,1024]{4,3,2,1,0:T(8,128)(2,1)}, bf16[2,4,4,32,1024]{4,3,2,1,0:T(8,128)(2,1)}) fusion(bf16[2,4,4,32,4096]{4,3,2,1,0:T(8,128)(2,1)S(1)} %bitcast.115), kind=kLoop, calls=%fused_computation.88 | loop fusion | bytes 16777216 | tf_op jit(solution)/shard_map/slice | solution.py:60
  178.8 1.4 copy-done.5
  180.2 0.8 dynamic-slice_bitcast_fusion.3
  181.0 0.7 collective-permute-start
  181.7 1.9 dynamic-slice_bitcast_fusion.2
  183.5 2.6 collective-permute-start.7
  186.1 1.2 dynamic-slice_bitcast_fusion.1
  187.3 0.8 collective-permute-start.14
  188.1 2.6 collective-permute-start.21
  190.7 5.6 %collective-permute-done = bf16[2,4,32,1024]{3,2,1,0:T(8,128)(2,1)S(1)} collective-permute-done((bf16[2,4,32,1024]{3,2,1,0:T(8,128)(2,1)}, bf16[2,4,32,1024]{3,2,1,0:T(8,128)(2,1)S(1)}, u32[]{:S(2)}, u32[]{:S(2)}) %collective-permute-start) | collective-permute-done | bytes 524320 | tf_op jit(solution)/shard_map/ppermute | solution.py:69
  196.3 1.1 bitcast_add_fusion.11
  197.6 3.7 %collective-permute-start.8 = (bf16[2,4,32,1024]{3,2,1,0:T(8,128)(2,1)S(1)}, bf16[2,4,32,1024]{3,2,1,0:T(8,128)(2,1)S(1)}, u32[]{:S(2)}, u32[]{:S(2)}) collective-permute-start(bf16[2,4,32,1024]{3,2,1,0:T(8,128)(2,1)S(1)} %bitcast_add_fusion.8), channel_id=1, source_target_pairs={{0,3},{1,0},{2,1},{3,2},{4,7},{5,4},{6,5},{7,6},{8,11},{9,8},{10,9... | collective-permute-start | bytes 1572872 | tf_op jit(solution)/shard_map/ppermute | solution.py:70
  201.3 0.7 collective-permute-done.14
  202.2 3.3 %collective-permute-start.22 = (bf16[2,4,32,1024]{3,2,1,0:T(8,128)(2,1)S(1)}, bf16[2,4,32,1024]{3,2,1,0:T(8,128)(2,1)S(1)}, u32[]{:S(2)}, u32[]{:S(2)}) collective-permute-start(bf16[2,4,32,1024]{3,2,1,0:T(8,128)(2,1)S(1)} %bitcast_add_fusion.2), channel_id=1, source_target_pairs={{0,12},{4,0},{8,4},{12,8},{1,13},{5,1},{9,5},{13,9},{2,14},{6,2},{... | collective-permute-start | bytes 1572872 | tf_op jit(solution)/shard_map/ppermute | solution.py:70
  205.5 6.3 %collective-permute-done.1 = bf16[2,4,32,1024]{3,2,1,0:T(8,128)(2,1)S(1)} collective-permute-done((bf16[2,4,32,1024]{3,2,1,0:T(8,128)(2,1)S(1)}, bf16[2,4,32,1024]{3,2,1,0:T(8,128)(2,1)S(1)}, u32[]{:S(2)}, u32[]{:S(2)}) %collective-permute-start.1) | collective-permute-done | bytes 524320 | tf_op jit(solution)/shard_map/ppermute | solution.py:69
  212.0 3.4 %collective-permute-start.9 = (bf16[2,4,32,1024]{3,2,1,0:T(8,128)(2,1)S(1)}, bf16[2,4,32,1024]{3,2,1,0:T(8,128)(2,1)S(1)}, u32[]{:S(2)}, u32[]{:S(2)}) collective-permute-start(bf16[2,4,32,1024]{3,2,1,0:T(8,128)(2,1)S(1)} %bitcast_add_fusion.7), channel_id=1, source_target_pairs={{0,3},{1,0},{2,1},{3,2},{4,7},{5,4},{6,5},{7,6},{8,11},{9,8},{10,9... | collective-permute-start | bytes 1572872 | tf_op jit(solution)/shard_map/ppermute | solution.py:70
  215.4 0.4 collective-permute-done.15
  216.0 3.3 %collective-permute-start.23 = (bf16[2,4,32,1024]{3,2,1,0:T(8,128)(2,1)S(1)}, bf16[2,4,32,1024]{3,2,1,0:T(8,128)(2,1)S(1)}, u32[]{:S(2)}, u32[]{:S(2)}) collective-permute-start(bf16[2,4,32,1024]{3,2,1,0:T(8,128)(2,1)S(1)} %bitcast_add_fusion.1), channel_id=1, source_target_pairs={{0,12},{4,0},{8,4},{12,8},{1,13},{5,1},{9,5},{13,9},{2,14},{6,2},{... | collective-permute-start | bytes 1572872 | tf_op jit(solution)/shard_map/ppermute | solution.py:70
  219.3 6.0 %collective-permute-done.2 = bf16[2,4,32,1024]{3,2,1,0:T(8,128)(2,1)S(1)} collective-permute-done((bf16[2,4,32,1024]{3,2,1,0:T(8,128)(2,1)S(1)}, bf16[2,4,32,1024]{3,2,1,0:T(8,128)(2,1)S(1)}, u32[]{:S(2)}, u32[]{:S(2)}) %collective-permute-start.2) | collective-permute-done | bytes 524320 | tf_op jit(solution)/shard_map/ppermute | solution.py:69
  225.6 3.3 %collective-permute-start.10 = (bf16[2,32,1024]{2,1,0:T(8,128)(2,1)S(1)}, bf16[2,32,1024]{2,1,0:T(8,128)(2,1)S(1)}, u32[]{:S(2)}, u32[]{:S(2)}) collective-permute-start(bf16[2,32,1024]{2,1,0:T(8,128)(2,1)S(1)} %dynamic-slice_bitcast_fusion.6), channel_id=1, source_target_pairs={{0,12},{4,0},{8,4},{12,8},{1,13},{5,1},{9,5},{13,9},{2,14},{6,2},{... | collective-permute-start | bytes 393224 | tf_op jit(solution)/shard_map/ppermute | solution.py:70
  228.9 1.3 collective-permute-done.16
  230.5 3.3 %collective-permute-start.24 = (bf16[2,32,1024]{2,1,0:T(8,128)(2,1)S(1)}, bf16[2,32,1024]{2,1,0:T(8,128)(2,1)S(1)}, u32[]{:S(2)}, u32[]{:S(2)}) collective-permute-start(bf16[2,32,1024]{2,1,0:T(8,128)(2,1)S(1)} %dynamic-slice_bitcast_fusion.4), channel_id=1, source_target_pairs={{0,3},{1,0},{2,1},{3,2},{4,7},{5,4},{6,5},{7,6},{8,11},{9,8},{10,9... | collective-permute-start | bytes 393224 | tf_op jit(solution)/shard_map/ppermute | solution.py:70
  233.9 3.3 %collective-permute-start.11 = (bf16[2,32,1024]{2,1,0:T(8,128)(2,1)S(1)}, bf16[2,32,1024]{2,1,0:T(8,128)(2,1)S(1)}, u32[]{:S(2)}, u32[]{:S(2)}) collective-permute-start(bf16[2,32,1024]{2,1,0:T(8,128)(2,1)S(1)} %bitcast_add_fusion.20), channel_id=1, source_target_pairs={{0,12},{4,0},{8,4},{12,8},{1,13},{5,1},{9,5},{13,9},{2,14},{6,2},{... | collective-permute-start | bytes 393224 | tf_op jit(solution)/shard_map/ppermute | solution.py:70
  237.3 3.3 %collective-permute-start.25 = (bf16[2,32,1024]{2,1,0:T(8,128)(2,1)S(1)}, bf16[2,32,1024]{2,1,0:T(8,128)(2,1)S(1)}, u32[]{:S(2)}, u32[]{:S(2)}) collective-permute-start(bf16[2,32,1024]{2,1,0:T(8,128)(2,1)S(1)} %bitcast_add_fusion.14), channel_id=1, source_target_pairs={{0,3},{1,0},{2,1},{3,2},{4,7},{5,4},{6,5},{7,6},{8,11},{9,8},{10,9... | collective-permute-start | bytes 393224 | tf_op jit(solution)/shard_map/ppermute | solution.py:70
  240.6 0.3 collective-permute-start.5
  241.0 3.3 %collective-permute-start.12 = (bf16[2,32,1024]{2,1,0:T(8,128)(2,1)S(1)}, bf16[2,32,1024]{2,1,0:T(8,128)(2,1)S(1)}, u32[]{:S(2)}, u32[]{:S(2)}) collective-permute-start(bf16[2,32,1024]{2,1,0:T(8,128)(2,1)S(1)} %bitcast_add_fusion.19), channel_id=1, source_target_pairs={{0,12},{4,0},{8,4},{12,8},{1,13},{5,1},{9,5},{13,9},{2,14},{6,2},{... | collective-permute-start | bytes 393224 | tf_op jit(solution)/shard_map/ppermute | solution.py:70
  244.2 0.2 collective-permute-done.18
  244.5 3.6 %collective-permute-start.26 = (bf16[2,32,1024]{2,1,0:T(8,128)(2,1)S(1)}, bf16[2,32,1024]{2,1,0:T(8,128)(2,1)S(1)}, u32[]{:S(2)}, u32[]{:S(2)}) collective-permute-start(bf16[2,32,1024]{2,1,0:T(8,128)(2,1)S(1)} %bitcast_add_fusion.13), channel_id=1, source_target_pairs={{0,3},{1,0},{2,1},{3,2},{4,7},{5,4},{6,5},{7,6},{8,11},{9,8},{10,9... | collective-permute-start | bytes 393224 | tf_op jit(solution)/shard_map/ppermute | solution.py:70
  248.1 0.1 collective-permute-start.6
  248.3 3.6 %collective-permute-start.13 = (bf16[32,1024]{1,0:T(8,128)(2,1)S(1)}, bf16[32,1024]{1,0:T(8,128)(2,1)S(1)}, u32[]{:S(2)}, u32[]{:S(2)}) collective-permute-start(bf16[32,1024]{1,0:T(8,128)(2,1)S(1)} %dynamic-slice_bitcast_fusion.10), channel_id=1, source_target_pairs={{0,16},{16,0},{1,17},{17,1},{2,18},{18,2},{3,19},{19,3},{4,20},{20... | collective-permute-start | bytes 196616 | tf_op jit(solution)/shard_map/ppermute | solution.py:70
  251.9 0.1 collective-permute-start.20
  252.1 3.6 %collective-permute-start.27 = (bf16[32,1024]{1,0:T(8,128)(2,1)S(1)}, bf16[32,1024]{1,0:T(8,128)(2,1)S(1)}, u32[]{:S(2)}, u32[]{:S(2)}) collective-permute-start(bf16[32,1024]{1,0:T(8,128)(2,1)S(1)} %dynamic-slice_bitcast_fusion.8), channel_id=1, source_target_pairs={{0,16},{16,0},{1,17},{17,1},{2,18},{18,2},{3,19},{19,3},{4,20},{20... | collective-permute-start | bytes 196616 | tf_op jit(solution)/shard_map/ppermute | solution.py:70
  255.7 2.1 collective-permute-done.20
  257.8 0.7 collective-permute-done.27
  258.5 0.7 pad_maximum_fusion.2
  (99 shorter events, 2.2 us)
Async XLA Ops:
  6.5 97.3 %copy-start = (bf16[4096,64]{0,1:T(8,128)(2,1)S(1)}, bf16[4096,64]{0,1:T(8,128)(2,1)}, u32[]{:S(2)}) copy-start(bf16[4096,64]{0,1:T(8,128)(2,1)} %param.11) | copy-start | bytes 1572868
  6.5 2.8 %copy-start.7 = (bf16[32,16384]{1,0:T(8,128)(2,1)S(1)}, bf16[32,16384]{1,0:T(8,128)(2,1)}, u32[]{:S(2)}) copy-start(bf16[32,16384]{1,0:T(8,128)(2,1)} %param.8) | copy-start | bytes 3145732
  6.5 88.0 %all-gather.2.cloned.1.call-start = ((), (), s32[]{:S(2)}) async-start(), calls=%async_computation.2 | async-start | bytes 8912896 | tf_op jit(solution)/shard_map/all_gather | solution.py:84
  6.5 3.2 %copy-start.8 = (bf16[16384]{0:T(1024)(128)(2,1)S(1)}, bf16[16384]{0:T(1024)(128)(2,1)}, u32[]{:S(2)}) copy-start(bf16[16384]{0:T(1024)(128)(2,1)} %param.9) | copy-start | bytes 98308
  94.6 9.3 %copy-start.2 = (bf16[1024,4096]{1,0:T(8,128)(2,1)S(1)}, bf16[1024,4096]{1,0:T(8,128)(2,1)}, u32[]{:S(2)}) copy-start(bf16[1024,4096]{1,0:T(8,128)(2,1)} %all-gather.2.cloned.1.call-done) | copy-start | bytes 25165828
  107.3 9.7 %copy-start.9 = (s32[8]{0:T(128)S(1)}, s32[8]{0:T(128)}, u32[]{:S(2)}) copy-start(s32[8]{0:T(128)} %param.14) | copy-start | bytes 100
  108.6 29.2 %all-to-all-start = ((bf16[128,8,576]{2,1,0:T(8,128)(2,1)}), bf16[128,8,576]{2,1,0:T(8,128)(2,1)S(1)}, u32[]{:S(2)}, u32[]{:S(2)}) async-start(bf16[128,8,576]{2,1,0:T(8,128)(2,1)} %bitcast.2), calls=%async_computation | async-start | bytes 2621440 | tf_op jit(solution)/shard_map/all_to_all | solution.py:94
  139.4 4.1 %copy-start.10 = (bf16[8,256,8,128]{3,2,1,0:T(8,128)(2,1)S(1)}, bf16[8,256,8,128]{3,2,1,0:T(8,128)(2,1)}, u32[]{:S(2)}) copy-start(bf16[8,256,8,128]{3,2,1,0:T(8,128)(2,1)} %param.13) | copy-start | bytes 12582916
  145.9 23.2 %all-to-all-start.1 = ((bf16[128,8,512]{2,1,0:T(8,128)(2,1)}), bf16[128,8,512]{2,1,0:T(8,128)(2,1)S(1)}, u32[]{:S(2)}, u32[]{:S(2)}) async-start(bf16[128,8,512]{2,1,0:T(8,128)(2,1)} %bitcast.14), calls=%async_computation.1 | async-start | bytes 2097152 | tf_op jit(solution)/shard_map/all_to_all | solution.py:103
  178.8 1.4 copy-start.5
  181.0 15.3 %collective-permute-start = (bf16[2,4,32,1024]{3,2,1,0:T(8,128)(2,1)}, bf16[2,4,32,1024]{3,2,1,0:T(8,128)(2,1)S(1)}, u32[]{:S(2)}, u32[]{:S(2)}) collective-permute-start(bf16[2,4,32,1024]{3,2,1,0:T(8,128)(2,1)} %dynamic-slice_bitcast_fusion.3), channel_id=1, source_target_pairs={{0,1},{1,2},{2,3},{3,0},{4,5},{5,6},{6,7},{7,4},{8,9},{9,10},{10,1... | collective-permute-start | bytes 1572872 | tf_op jit(solution)/shard_map/ppermute | solution.py:69
  183.5 14.0 %collective-permute-start.7 = (bf16[2,4,32,1024]{3,2,1,0:T(8,128)(2,1)}, bf16[2,4,32,1024]{3,2,1,0:T(8,128)(2,1)S(1)}, u32[]{:S(2)}, u32[]{:S(2)}) collective-permute-start(bf16[2,4,32,1024]{3,2,1,0:T(8,128)(2,1)} %dynamic-slice_bitcast_fusion.2), channel_id=1, source_target_pairs={{0,3},{1,0},{2,1},{3,2},{4,7},{5,4},{6,5},{7,6},{8,11},{9,8},{10,9... | collective-permute-start | bytes 1572872 | tf_op jit(solution)/shard_map/ppermute | solution.py:70
  186.1 11.5 %copy-start.4 = (bf16[2,4,4,32,1024]{4,3,2,1,0:T(8,128)(2,1)S(1)}, bf16[2,4,4,32,1024]{4,3,2,1,0:T(8,128)(2,1)}, u32[]{:S(2)}) copy-start(bf16[2,4,4,32,1024]{4,3,2,1,0:T(8,128)(2,1)} %get-tuple-element.8) | copy-start | bytes 6291460
  187.3 14.6 %collective-permute-start.14 = (bf16[2,4,32,1024]{3,2,1,0:T(8,128)(2,1)S(1)}, bf16[2,4,32,1024]{3,2,1,0:T(8,128)(2,1)S(1)}, u32[]{:S(2)}, u32[]{:S(2)}) collective-permute-start(bf16[2,4,32,1024]{3,2,1,0:T(8,128)(2,1)S(1)} %dynamic-slice_bitcast_fusion.1), channel_id=1, source_target_pairs={{0,4},{4,8},{8,12},{12,0},{1,5},{5,9},{9,13},{13,1},{2,6},{6,10},{... | collective-permute-start | bytes 1572872 | tf_op jit(solution)/shard_map/ppermute | solution.py:69
  188.1 13.9 %copy-start.3 = (bf16[2,4,4,32,1024]{4,3,2,1,0:T(8,128)(2,1)S(1)}, bf16[2,4,4,32,1024]{4,3,2,1,0:T(8,128)(2,1)}, u32[]{:S(2)}) copy-start(bf16[2,4,4,32,1024]{4,3,2,1,0:T(8,128)(2,1)} %get-tuple-element.7) | copy-start | bytes 6291460
  188.1 14.0 %collective-permute-start.21 = (bf16[2,4,32,1024]{3,2,1,0:T(8,128)(2,1)S(1)}, bf16[2,4,32,1024]{3,2,1,0:T(8,128)(2,1)S(1)}, u32[]{:S(2)}, u32[]{:S(2)}) collective-permute-start(bf16[2,4,32,1024]{3,2,1,0:T(8,128)(2,1)S(1)} %dynamic-slice_bitcast_fusion), channel_id=1, source_target_pairs={{0,12},{4,0},{8,4},{12,8},{1,13},{5,1},{9,5},{13,9},{2,14},{6,2},{... | collective-permute-start | bytes 1572872 | tf_op jit(solution)/shard_map/ppermute | solution.py:70
  197.4 14.3 %copy-start.6 = (bf16[2,4,4,32,1024]{4,3,2,1,0:T(8,128)(2,1)S(1)}, bf16[2,4,4,32,1024]{4,3,2,1,0:T(8,128)(2,1)}, u32[]{:S(2)}) copy-start(bf16[2,4,4,32,1024]{4,3,2,1,0:T(8,128)(2,1)} %copy-done.5) | copy-start | bytes 6291460
  197.4 14.3 %collective-permute-start.1 = (bf16[2,4,32,1024]{3,2,1,0:T(8,128)(2,1)S(1)}, bf16[2,4,32,1024]{3,2,1,0:T(8,128)(2,1)S(1)}, u32[]{:S(2)}, u32[]{:S(2)}) collective-permute-start(bf16[2,4,32,1024]{3,2,1,0:T(8,128)(2,1)S(1)} %bitcast_add_fusion.11), channel_id=1, source_target_pairs={{0,1},{1,2},{2,3},{3,0},{4,5},{5,6},{6,7},{7,4},{8,9},{9,10},{10,1... | collective-permute-start | bytes 1572872 | tf_op jit(solution)/shard_map/ppermute | solution.py:69
  197.6 14.3 %collective-permute-start.8 = (bf16[2,4,32,1024]{3,2,1,0:T(8,128)(2,1)S(1)}, bf16[2,4,32,1024]{3,2,1,0:T(8,128)(2,1)S(1)}, u32[]{:S(2)}, u32[]{:S(2)}) collective-permute-start(bf16[2,4,32,1024]{3,2,1,0:T(8,128)(2,1)S(1)} %bitcast_add_fusion.8), channel_id=1, source_target_pairs={{0,3},{1,0},{2,1},{3,2},{4,7},{5,4},{6,5},{7,6},{8,11},{9,8},{10,9... | collective-permute-start | bytes 1572872 | tf_op jit(solution)/shard_map/ppermute | solution.py:70
  202.0 13.8 %collective-permute-start.15 = (bf16[2,4,32,1024]{3,2,1,0:T(8,128)(2,1)S(1)}, bf16[2,4,32,1024]{3,2,1,0:T(8,128)(2,1)S(1)}, u32[]{:S(2)}, u32[]{:S(2)}) collective-permute-start(bf16[2,4,32,1024]{3,2,1,0:T(8,128)(2,1)S(1)} %bitcast_add_fusion.5), channel_id=1, source_target_pairs={{0,4},{4,8},{8,12},{12,0},{1,5},{5,9},{9,13},{13,1},{2,6},{6,10},{... | collective-permute-start | bytes 1572872 | tf_op jit(solution)/shard_map/ppermute | solution.py:69
  202.2 13.8 %collective-permute-start.22 = (bf16[2,4,32,1024]{3,2,1,0:T(8,128)(2,1)S(1)}, bf16[2,4,32,1024]{3,2,1,0:T(8,128)(2,1)S(1)}, u32[]{:S(2)}, u32[]{:S(2)}) collective-permute-start(bf16[2,4,32,1024]{3,2,1,0:T(8,128)(2,1)S(1)} %bitcast_add_fusion.2), channel_id=1, source_target_pairs={{0,12},{4,0},{8,4},{12,8},{1,13},{5,1},{9,5},{13,9},{2,14},{6,2},{... | collective-permute-start | bytes 1572872 | tf_op jit(solution)/shard_map/ppermute | solution.py:70
  211.8 13.5 %collective-permute-start.2 = (bf16[2,4,32,1024]{3,2,1,0:T(8,128)(2,1)S(1)}, bf16[2,4,32,1024]{3,2,1,0:T(8,128)(2,1)S(1)}, u32[]{:S(2)}, u32[]{:S(2)}) collective-permute-start(bf16[2,4,32,1024]{3,2,1,0:T(8,128)(2,1)S(1)} %bitcast_add_fusion.10), channel_id=1, source_target_pairs={{0,1},{1,2},{2,3},{3,0},{4,5},{5,6},{6,7},{7,4},{8,9},{9,10},{10,1... | collective-permute-start | bytes 1572872 | tf_op jit(solution)/shard_map/ppermute | solution.py:69
  212.0 13.5 %collective-permute-start.9 = (bf16[2,4,32,1024]{3,2,1,0:T(8,128)(2,1)S(1)}, bf16[2,4,32,1024]{3,2,1,0:T(8,128)(2,1)S(1)}, u32[]{:S(2)}, u32[]{:S(2)}) collective-permute-start(bf16[2,4,32,1024]{3,2,1,0:T(8,128)(2,1)S(1)} %bitcast_add_fusion.7), channel_id=1, source_target_pairs={{0,3},{1,0},{2,1},{3,2},{4,7},{5,4},{6,5},{7,6},{8,11},{9,8},{10,9... | collective-permute-start | bytes 1572872 | tf_op jit(solution)/shard_map/ppermute | solution.py:70
  215.9 14.3 %collective-permute-start.16 = (bf16[2,4,32,1024]{3,2,1,0:T(8,128)(2,1)S(1)}, bf16[2,4,32,1024]{3,2,1,0:T(8,128)(2,1)S(1)}, u32[]{:S(2)}, u32[]{:S(2)}) collective-permute-start(bf16[2,4,32,1024]{3,2,1,0:T(8,128)(2,1)S(1)} %bitcast_add_fusion.4), channel_id=1, source_target_pairs={{0,4},{4,8},{8,12},{12,0},{1,5},{5,9},{9,13},{13,1},{2,6},{6,10},{... | collective-permute-start | bytes 1572872 | tf_op jit(solution)/shard_map/ppermute | solution.py:69
  216.0 14.3 %collective-permute-start.23 = (bf16[2,4,32,1024]{3,2,1,0:T(8,128)(2,1)S(1)}, bf16[2,4,32,1024]{3,2,1,0:T(8,128)(2,1)S(1)}, u32[]{:S(2)}, u32[]{:S(2)}) collective-permute-start(bf16[2,4,32,1024]{3,2,1,0:T(8,128)(2,1)S(1)} %bitcast_add_fusion.1), channel_id=1, source_target_pairs={{0,12},{4,0},{8,4},{12,8},{1,13},{5,1},{9,5},{13,9},{2,14},{6,2},{... | collective-permute-start | bytes 1572872 | tf_op jit(solution)/shard_map/ppermute | solution.py:70
  225.4 8.3 %collective-permute-start.3 = (bf16[2,32,1024]{2,1,0:T(8,128)(2,1)S(1)}, bf16[2,32,1024]{2,1,0:T(8,128)(2,1)S(1)}, u32[]{:S(2)}, u32[]{:S(2)}) collective-permute-start(bf16[2,32,1024]{2,1,0:T(8,128)(2,1)S(1)} %dynamic-slice_bitcast_fusion.7), channel_id=1, source_target_pairs={{0,4},{4,8},{8,12},{12,0},{1,5},{5,9},{9,13},{13,1},{2,6},{6,10},{... | collective-permute-start | bytes 393224 | tf_op jit(solution)/shard_map/ppermute | solution.py:69
  225.6 8.3 %collective-permute-start.10 = (bf16[2,32,1024]{2,1,0:T(8,128)(2,1)S(1)}, bf16[2,32,1024]{2,1,0:T(8,128)(2,1)S(1)}, u32[]{:S(2)}, u32[]{:S(2)}) collective-permute-start(bf16[2,32,1024]{2,1,0:T(8,128)(2,1)S(1)} %dynamic-slice_bitcast_fusion.6), channel_id=1, source_target_pairs={{0,12},{4,0},{8,4},{12,8},{1,13},{5,1},{9,5},{13,9},{2,14},{6,2},{... | collective-permute-start | bytes 393224 | tf_op jit(solution)/shard_map/ppermute | solution.py:70
  230.3 6.9 %collective-permute-start.17 = (bf16[2,32,1024]{2,1,0:T(8,128)(2,1)S(1)}, bf16[2,32,1024]{2,1,0:T(8,128)(2,1)S(1)}, u32[]{:S(2)}, u32[]{:S(2)}) collective-permute-start(bf16[2,32,1024]{2,1,0:T(8,128)(2,1)S(1)} %dynamic-slice_bitcast_fusion.5), channel_id=1, source_target_pairs={{0,1},{1,2},{2,3},{3,0},{4,5},{5,6},{6,7},{7,4},{8,9},{9,10},{10,1... | collective-permute-start | bytes 393224 | tf_op jit(solution)/shard_map/ppermute | solution.py:69
  230.5 6.8 %collective-permute-start.24 = (bf16[2,32,1024]{2,1,0:T(8,128)(2,1)S(1)}, bf16[2,32,1024]{2,1,0:T(8,128)(2,1)S(1)}, u32[]{:S(2)}, u32[]{:S(2)}) collective-permute-start(bf16[2,32,1024]{2,1,0:T(8,128)(2,1)S(1)} %dynamic-slice_bitcast_fusion.4), channel_id=1, source_target_pairs={{0,3},{1,0},{2,1},{3,2},{4,7},{5,4},{6,5},{7,6},{8,11},{9,8},{10,9... | collective-permute-start | bytes 393224 | tf_op jit(solution)/shard_map/ppermute | solution.py:70
  233.8 6.8 %collective-permute-start.4 = (bf16[2,32,1024]{2,1,0:T(8,128)(2,1)S(1)}, bf16[2,32,1024]{2,1,0:T(8,128)(2,1)S(1)}, u32[]{:S(2)}, u32[]{:S(2)}) collective-permute-start(bf16[2,32,1024]{2,1,0:T(8,128)(2,1)S(1)} %bitcast_add_fusion.23), channel_id=1, source_target_pairs={{0,4},{4,8},{8,12},{12,0},{1,5},{5,9},{9,13},{13,1},{2,6},{6,10},{... | collective-permute-start | bytes 393224 | tf_op jit(solution)/shard_map/ppermute | solution.py:69
  233.9 7.0 %collective-permute-start.11 = (bf16[2,32,1024]{2,1,0:T(8,128)(2,1)S(1)}, bf16[2,32,1024]{2,1,0:T(8,128)(2,1)S(1)}, u32[]{:S(2)}, u32[]{:S(2)}) collective-permute-start(bf16[2,32,1024]{2,1,0:T(8,128)(2,1)S(1)} %bitcast_add_fusion.20), channel_id=1, source_target_pairs={{0,12},{4,0},{8,4},{12,8},{1,13},{5,1},{9,5},{13,9},{2,14},{6,2},{... | collective-permute-start | bytes 393224 | tf_op jit(solution)/shard_map/ppermute | solution.py:70
  237.2 7.2 %collective-permute-start.18 = (bf16[2,32,1024]{2,1,0:T(8,128)(2,1)S(1)}, bf16[2,32,1024]{2,1,0:T(8,128)(2,1)S(1)}, u32[]{:S(2)}, u32[]{:S(2)}) collective-permute-start(bf16[2,32,1024]{2,1,0:T(8,128)(2,1)S(1)} %bitcast_add_fusion.17), channel_id=1, source_target_pairs={{0,1},{1,2},{2,3},{3,0},{4,5},{5,6},{6,7},{7,4},{8,9},{9,10},{10,1... | collective-permute-start | bytes 393224 | tf_op jit(solution)/shard_map/ppermute | solution.py:69
  237.3 7.2 %collective-permute-start.25 = (bf16[2,32,1024]{2,1,0:T(8,128)(2,1)S(1)}, bf16[2,32,1024]{2,1,0:T(8,128)(2,1)S(1)}, u32[]{:S(2)}, u32[]{:S(2)}) collective-permute-start(bf16[2,32,1024]{2,1,0:T(8,128)(2,1)S(1)} %bitcast_add_fusion.14), channel_id=1, source_target_pairs={{0,3},{1,0},{2,1},{3,2},{4,7},{5,4},{6,5},{7,6},{8,11},{9,8},{10,9... | collective-permute-start | bytes 393224 | tf_op jit(solution)/shard_map/ppermute | solution.py:70
  240.6 7.5 %collective-permute-start.5 = (bf16[2,32,1024]{2,1,0:T(8,128)(2,1)S(1)}, bf16[2,32,1024]{2,1,0:T(8,128)(2,1)S(1)}, u32[]{:S(2)}, u32[]{:S(2)}) collective-permute-start(bf16[2,32,1024]{2,1,0:T(8,128)(2,1)S(1)} %bitcast_add_fusion.22), channel_id=1, source_target_pairs={{0,4},{4,8},{8,12},{12,0},{1,5},{5,9},{9,13},{13,1},{2,6},{6,10},{... | collective-permute-start | bytes 393224 | tf_op jit(solution)/shard_map/ppermute | solution.py:69
  240.9 18.3 %copy-start.1 = (bf16[4096,64]{0,1:T(8,128)(2,1)S(1)}, bf16[4096,64]{0,1:T(8,128)(2,1)}, u32[]{:S(2)}) copy-start(bf16[4096,64]{0,1:T(8,128)(2,1)} %param.11) | copy-start | bytes 1572868
  241.0 7.3 %collective-permute-start.12 = (bf16[2,32,1024]{2,1,0:T(8,128)(2,1)S(1)}, bf16[2,32,1024]{2,1,0:T(8,128)(2,1)S(1)}, u32[]{:S(2)}, u32[]{:S(2)}) collective-permute-start(bf16[2,32,1024]{2,1,0:T(8,128)(2,1)S(1)} %bitcast_add_fusion.19), channel_id=1, source_target_pairs={{0,12},{4,0},{8,4},{12,8},{1,13},{5,1},{9,5},{13,9},{2,14},{6,2},{... | collective-permute-start | bytes 393224 | tf_op jit(solution)/shard_map/ppermute | solution.py:70
  244.4 7.5 %collective-permute-start.19 = (bf16[2,32,1024]{2,1,0:T(8,128)(2,1)S(1)}, bf16[2,32,1024]{2,1,0:T(8,128)(2,1)S(1)}, u32[]{:S(2)}, u32[]{:S(2)}) collective-permute-start(bf16[2,32,1024]{2,1,0:T(8,128)(2,1)S(1)} %bitcast_add_fusion.16), channel_id=1, source_target_pairs={{0,1},{1,2},{2,3},{3,0},{4,5},{5,6},{6,7},{7,4},{8,9},{9,10},{10,1... | collective-permute-start | bytes 393224 | tf_op jit(solution)/shard_map/ppermute | solution.py:69
  244.5 7.5 %collective-permute-start.26 = (bf16[2,32,1024]{2,1,0:T(8,128)(2,1)S(1)}, bf16[2,32,1024]{2,1,0:T(8,128)(2,1)S(1)}, u32[]{:S(2)}, u32[]{:S(2)}) collective-permute-start(bf16[2,32,1024]{2,1,0:T(8,128)(2,1)S(1)} %bitcast_add_fusion.13), channel_id=1, source_target_pairs={{0,3},{1,0},{2,1},{3,2},{4,7},{5,4},{6,5},{7,6},{8,11},{9,8},{10,9... | collective-permute-start | bytes 393224 | tf_op jit(solution)/shard_map/ppermute | solution.py:70
  248.1 7.5 %collective-permute-start.6 = (bf16[32,1024]{1,0:T(8,128)(2,1)S(1)}, bf16[32,1024]{1,0:T(8,128)(2,1)S(1)}, u32[]{:S(2)}, u32[]{:S(2)}) collective-permute-start(bf16[32,1024]{1,0:T(8,128)(2,1)S(1)} %dynamic-slice_bitcast_fusion.11), channel_id=1, source_target_pairs={{0,16},{16,0},{1,17},{17,1},{2,18},{18,2},{3,19},{19,3},{4,20},{20... | collective-permute-start | bytes 196616 | tf_op jit(solution)/shard_map/ppermute | solution.py:69
  248.3 9.5 %collective-permute-start.13 = (bf16[32,1024]{1,0:T(8,128)(2,1)S(1)}, bf16[32,1024]{1,0:T(8,128)(2,1)S(1)}, u32[]{:S(2)}, u32[]{:S(2)}) collective-permute-start(bf16[32,1024]{1,0:T(8,128)(2,1)S(1)} %dynamic-slice_bitcast_fusion.10), channel_id=1, source_target_pairs={{0,16},{16,0},{1,17},{17,1},{2,18},{18,2},{3,19},{19,3},{4,20},{20... | collective-permute-start | bytes 196616 | tf_op jit(solution)/shard_map/ppermute | solution.py:70
  251.9 5.8 %collective-permute-start.20 = (bf16[32,1024]{1,0:T(8,128)(2,1)S(1)}, bf16[32,1024]{1,0:T(8,128)(2,1)S(1)}, u32[]{:S(2)}, u32[]{:S(2)}) collective-permute-start(bf16[32,1024]{1,0:T(8,128)(2,1)S(1)} %dynamic-slice_bitcast_fusion.9), channel_id=1, source_target_pairs={{0,16},{16,0},{1,17},{17,1},{2,18},{18,2},{3,19},{19,3},{4,20},{20... | collective-permute-start | bytes 196616 | tf_op jit(solution)/shard_map/ppermute | solution.py:69
  252.1 6.4 %collective-permute-start.27 = (bf16[32,1024]{1,0:T(8,128)(2,1)S(1)}, bf16[32,1024]{1,0:T(8,128)(2,1)S(1)}, u32[]{:S(2)}, u32[]{:S(2)}) collective-permute-start(bf16[32,1024]{1,0:T(8,128)(2,1)S(1)} %dynamic-slice_bitcast_fusion.8), channel_id=1, source_target_pairs={{0,16},{16,0},{1,17},{17,1},{2,18},{18,2},{3,19},{19,3},{4,20},{20... | collective-permute-start | bytes 196616 | tf_op jit(solution)/shard_map/ppermute | solution.py:70
Sparse Core Ops, SparseCore 0:
  22.1 72.4 all-gather.1
